TPU v7x, 32 devices: a whole 2x2x4 slice. The times are simulated.
32 devices in a mesh: fsdp: 4 (over x, core), replica: 8 (over z, y).
Axes of the slice: x: 2, y: 2, z: 4, core: 2. Of those that a mesh axis runs over, the one named last changes fastest.
Arguments:
- hidden_in: bfloat16 [16384, 768], P(('fsdp', 'replica')), may hold values from -6 to 6
- encoder_states: bfloat16 [16384, 768], P(('fsdp', 'replica')), may hold values from -6 to 6
- output_grad: bfloat16 [16384, 768], P(('fsdp', 'replica')), may hold values from -6 to 6
- piece_starts: int32 [32, 3], P(('fsdp', 'replica')), may hold values from 0 to 384, as said below
- selfquery: bfloat16 [768, 768], P('fsdp'), may hold values from -0.0546875 to 0.0546875
- selfkey: bfloat16 [768, 768], P('fsdp'), may hold values from -0.21875 to 0.21875
- selfvalue: bfloat16 [768, 768], P('fsdp'), may hold values from -0.21875 to 0.21875
- selfproj: bfloat16 [768, 768], P('fsdp'), may hold values from -0.875 to 0.875
- crossquery: bfloat16 [768, 768], P('fsdp'), may hold values from -0.0546875 to 0.0546875
- crosskey: bfloat16 [768, 768], P('fsdp'), may hold values from -0.21875 to 0.21875
- crossvalue: bfloat16 [768, 768], P('fsdp'), may hold values from -0.21875 to 0.21875
- crossproj: bfloat16 [768, 768], P('fsdp'), may hold values from -0.875 to 0.875
- gateproj: bfloat16 [768, 2048], P('fsdp'), may hold values from -0.21875 to 0.21875
- upproj: bfloat16 [768, 2048], P('fsdp'), may hold values from -0.21875 to 0.21875
- downproj: bfloat16 [2048, 768], P('fsdp'), may hold values from -0.125 to 0.125
- gainself: bfloat16 [768], P('fsdp'), may hold values from 0.5 to 1.5
- gaincross: bfloat16 [768], P('fsdp'), may hold values from 0.5 to 1.5
- gainffn: bfloat16 [768], P('fsdp'), may hold values from 0.5 to 1.5
- reltable: bfloat16 [32, 12], P('fsdp'), may hold values from -4 to 4
Outputs:
- layer_out: bfloat16 [16384, 768], P(('fsdp', 'replica'))
- hidden_grad: float32 [16384, 768], P(('fsdp', 'replica'))
- encoder_grad: float32 [16384, 768], P(('fsdp', 'replica'))
- selfquery_grad: float32 [768, 768], P('fsdp')
- selfkey_grad: float32 [768, 768], P('fsdp')
- selfvalue_grad: float32 [768, 768], P('fsdp')
- selfproj_grad: float32 [768, 768], P('fsdp')
- crossquery_grad: float32 [768, 768], P('fsdp')
- crosskey_grad: float32 [768, 768], P('fsdp')
- crossvalue_grad: float32 [768, 768], P('fsdp')
- crossproj_grad: float32 [768, 768], P('fsdp')
- gateproj_grad: float32 [768, 2048], P('fsdp')
- upproj_grad: float32 [768, 2048], P('fsdp')
- downproj_grad: float32 [2048, 768], P('fsdp')
- gainself_grad: float32 [768], P('fsdp')
- gaincross_grad: float32 [768], P('fsdp')
- gainffn_grad: float32 [768], P('fsdp')
- reltable_grad: float32 [32, 12], P('fsdp')
Inputs may be any that keep to these rules, and one draw needn't show every extreme that they name: `piece_starts`: each row holds the 3 increasing starts of one sequence's pieces, the first 0 and the last exactly 384; no piece has more than 256 tokens, and each sequence has one piece of exactly 256.
All inputs are finite; a program needn't handle non-finite values.
Results may differ from a plain program's by a relative error of at most 0.028.
The roundings to bfloat16 on the way count: a program that leaves them out, or rounds other values in their place, can miss the bound.
Values may be sent and summed in bfloat16 or wider, within the bound.
No kernel may reach another device: no remote copies, remote signals or barrier semaphores. Data moves between devices by JAX's collectives and lax.ppermute only.
A program may use at most 256 MiB of HBM per device.

v0:
```python
import jax
import jax.numpy as jnp
from jax import lax
from jax.sharding import PartitionSpec as P

HEADS = 12
HEAD_DIM = 64
BUCKETS = 32
QBLOCK = 512


EPS = 1e-06
NEG = -1000000000.0
EDGES = (1, 2, 3, 4, 5, 6, 7, 8, 12, 16, 23, 32, 46, 64, 91)


def rms_scale(hidden, gain):
    return hidden * lax.rsqrt(jnp.mean(hidden * hidden, axis=-1, keepdims=True) + EPS) * gain


def gated(gate, upper):
    return jax.nn.gelu(gate, approximate=True) * upper


def product(left, right):
    return jnp.dot(left, right, preferred_element_type=jnp.float32)


def left_product(left, right):
    return lax.dot_general(
        left, right, (((0,), (0,)), ((), ())), preferred_element_type=jnp.float32
    )


def right_product(left, right):
    return lax.dot_general(
        left, right, (((1,), (1,)), ((), ())), preferred_element_type=jnp.float32
    )


def split_heads(matrix):
    return matrix.reshape(matrix.shape[0], HEADS, HEAD_DIM)


def block_terms(context, block_rows, key_count):
    if context is None:
        return (None, None, None)
    rel_table, piece_ids = context
    query_pos = jnp.arange(block_rows, dtype=jnp.int32)
    key_pos = jnp.arange(key_count, dtype=jnp.int32)
    relative = key_pos[None, :] - query_pos[:, None]
    distance = jnp.abs(relative)
    bucket = 16 * (relative > 0).astype(jnp.int32)
    for edge_len in EDGES:
        bucket = bucket + (distance >= edge_len).astype(jnp.int32)
    onehot = (bucket[:, :, None] == jnp.arange(BUCKETS, dtype=jnp.int32)[None, None, :]).astype(
        jnp.bfloat16
    )
    bias_block = jnp.einsum("qkb,bh->hqk", onehot, rel_table, preferred_element_type=jnp.float32)
    allowed = (key_pos[None, :] <= query_pos[:, None]) | (piece_ids[None, :] == piece_ids[:, None])
    return (onehot, bias_block, allowed)


def block_scores(query_block, key_heads, bias_block, allowed):
    scores = jnp.einsum("qhd,khd->hqk", query_block, key_heads, preferred_element_type=jnp.float32)
    if bias_block is not None:
        scores = jnp.where(allowed[None], scores + bias_block, NEG)
    return scores


def attend_forward(queries, key_rows, value_rows, context):
    key_heads = split_heads(key_rows)
    value_heads = split_heads(value_rows)
    query_block = split_heads(queries)
    onehot, bias_block, allowed = block_terms(context, QBLOCK, key_rows.shape[0])
    scores = block_scores(query_block, key_heads, bias_block, allowed)
    row_max = jnp.max(scores, axis=-1, keepdims=True)
    raised = jnp.exp(scores - row_max)
    row_sum = jnp.sum(raised, axis=-1, keepdims=True)
    prob_low = (raised / row_sum).astype(jnp.bfloat16)
    mixed_block = jnp.einsum(
        "hqk,khd->qhd", prob_low, value_heads, preferred_element_type=jnp.float32
    )
    mixed_parts = mixed_block.reshape(QBLOCK, HEADS * HEAD_DIM).astype(jnp.bfloat16)
    lse_parts = row_max + jnp.log(row_sum)
    return (mixed_parts, lse_parts)


def attend_backward(queries, key_rows, value_rows, grad_mixed, lse_rows, context):
    key_count = key_rows.shape[0]
    key_heads = split_heads(key_rows)
    value_heads = split_heads(value_rows)
    table_grad = jnp.zeros((BUCKETS, HEADS), jnp.float32)
    query_block = split_heads(queries)
    grad_block = split_heads(grad_mixed)
    onehot, bias_block, allowed = block_terms(context, QBLOCK, key_count)
    scores = block_scores(query_block, key_heads, bias_block, allowed)
    probs = jnp.exp(scores - lse_rows)
    prob_low = probs.astype(jnp.bfloat16)
    grad_probs = jnp.einsum(
        "qhd,khd->hqk", grad_block, value_heads, preferred_element_type=jnp.float32
    )
    inner_sum = jnp.sum(probs * grad_probs, axis=-1, keepdims=True)
    grad_scores = (probs * (grad_probs - inner_sum)).astype(jnp.bfloat16)
    query_grad = jnp.einsum(
        "hqk,khd->qhd", grad_scores, key_heads, preferred_element_type=jnp.float32
    )
    query_parts = query_grad.reshape(QBLOCK, HEADS * HEAD_DIM).astype(jnp.bfloat16)
    key_grad = jnp.einsum(
        "hqk,qhd->khd", grad_scores, query_block, preferred_element_type=jnp.float32
    )
    value_grad = jnp.einsum(
        "hqk,qhd->khd", prob_low, grad_block, preferred_element_type=jnp.float32
    )
    if onehot is not None:
        table_grad = jnp.einsum(
            "hqk,qkb->bh", grad_scores, onehot, preferred_element_type=jnp.float32
        )
    key_low = key_grad.reshape(key_count, HEADS * HEAD_DIM).astype(jnp.bfloat16)
    value_low = value_grad.reshape(key_count, HEADS * HEAD_DIM).astype(jnp.bfloat16)
    return (query_parts, key_low, value_low, table_grad)


def on_device(
    hidden_in,
    encoder_states,
    output_grad,
    piece_starts,
    selfquery,
    selfkey,
    selfvalue,
    selfproj,
    crossquery,
    crosskey,
    crossvalue,
    crossproj,
    gateproj,
    upproj,
    downproj,
    gainself,
    gaincross,
    gainffn,
    reltable,
):
    (
        self_query,
        self_key,
        self_value,
        self_proj,
        cross_query,
        cross_key,
        cross_value,
        cross_proj,
        gate_full,
        up_full,
        down_full,
        gain_one,
        gain_two,
        gain_three,
        table_full,
    ) = (
        lax.all_gather(selfquery, "fsdp", axis=0, tiled=True),
        lax.all_gather(selfkey, "fsdp", axis=0, tiled=True),
        lax.all_gather(selfvalue, "fsdp", axis=0, tiled=True),
        lax.all_gather(selfproj, "fsdp", axis=0, tiled=True),
        lax.all_gather(crossquery, "fsdp", axis=0, tiled=True),
        lax.all_gather(crosskey, "fsdp", axis=0, tiled=True),
        lax.all_gather(crossvalue, "fsdp", axis=0, tiled=True),
        lax.all_gather(crossproj, "fsdp", axis=0, tiled=True),
        lax.all_gather(gateproj, "fsdp", axis=0, tiled=True),
        lax.all_gather(upproj, "fsdp", axis=0, tiled=True),
        lax.all_gather(downproj, "fsdp", axis=0, tiled=True),
        lax.all_gather(gainself, "fsdp", axis=0, tiled=True),
        lax.all_gather(gaincross, "fsdp", axis=0, tiled=True),
        lax.all_gather(gainffn, "fsdp", axis=0, tiled=True),
        lax.all_gather(reltable, "fsdp", axis=0, tiled=True),
    )
    length = hidden_in.shape[0]
    position = jnp.arange(length, dtype=jnp.int32)
    piece_ids = (
        jnp.sum((piece_starts[0][None, :] <= position[:, None]).astype(jnp.int32), axis=1) - 1
    )
    context = (table_full, piece_ids)
    resid_in = hidden_in.astype(jnp.float32)
    normed_one = rms_scale(resid_in, gain_one.astype(jnp.float32)).astype(jnp.bfloat16)
    query_one = product(normed_one, self_query).astype(jnp.bfloat16)
    key_one = product(normed_one, self_key).astype(jnp.bfloat16)
    value_one = product(normed_one, self_value).astype(jnp.bfloat16)
    mixed_one, lse_one = attend_forward(query_one, key_one, value_one, context)
    after_self = resid_in + product(mixed_one, self_proj)
    normed_two = rms_scale(after_self, gain_two.astype(jnp.float32)).astype(jnp.bfloat16)
    query_two = product(normed_two, cross_query).astype(jnp.bfloat16)
    key_two = product(encoder_states, cross_key).astype(jnp.bfloat16)
    value_two = product(encoder_states, cross_value).astype(jnp.bfloat16)
    mixed_two, lse_two = attend_forward(query_two, key_two, value_two, None)
    after_cross = after_self + product(mixed_two, cross_proj)
    normed_three = rms_scale(after_cross, gain_three.astype(jnp.float32)).astype(jnp.bfloat16)
    gate_pre = product(normed_three, gate_full)
    upper_pre = product(normed_three, up_full)
    inner = gated(gate_pre, upper_pre).astype(jnp.bfloat16)
    layer_out = (after_cross + product(inner, down_full)).astype(jnp.bfloat16)
    (
        self_query,
        self_key,
        self_value,
        self_proj,
        cross_query,
        cross_key,
        cross_value,
        cross_proj,
        gate_full,
        up_full,
        down_full,
        gain_one,
        gain_two,
        gain_three,
        table_full,
    ) = (
        lax.all_gather(selfquery, "fsdp", axis=0, tiled=True),
        lax.all_gather(selfkey, "fsdp", axis=0, tiled=True),
        lax.all_gather(selfvalue, "fsdp", axis=0, tiled=True),
        lax.all_gather(selfproj, "fsdp", axis=0, tiled=True),
        lax.all_gather(crossquery, "fsdp", axis=0, tiled=True),
        lax.all_gather(crosskey, "fsdp", axis=0, tiled=True),
        lax.all_gather(crossvalue, "fsdp", axis=0, tiled=True),
        lax.all_gather(crossproj, "fsdp", axis=0, tiled=True),
        lax.all_gather(gateproj, "fsdp", axis=0, tiled=True),
        lax.all_gather(upproj, "fsdp", axis=0, tiled=True),
        lax.all_gather(downproj, "fsdp", axis=0, tiled=True),
        lax.all_gather(gainself, "fsdp", axis=0, tiled=True),
        lax.all_gather(gaincross, "fsdp", axis=0, tiled=True),
        lax.all_gather(gainffn, "fsdp", axis=0, tiled=True),
        lax.all_gather(reltable, "fsdp", axis=0, tiled=True),
    )
    context = (table_full, piece_ids)
    downproj_grad = left_product(inner, output_grad)
    inner_grad = right_product(output_grad, down_full)
    gated_value, pull_gate = jax.vjp(gated, gate_pre, upper_pre)
    gate_grad, upper_grad = pull_gate(inner_grad)
    gate_low = gate_grad.astype(jnp.bfloat16)
    upper_low = upper_grad.astype(jnp.bfloat16)
    gateproj_grad = left_product(normed_three, gate_low)
    upproj_grad = left_product(normed_three, upper_low)
    normed_grad = right_product(gate_low, gate_full) + right_product(upper_low, up_full)
    norm_value, pull_norm = jax.vjp(rms_scale, after_cross, gain_three.astype(jnp.float32))
    back_resid, gainffn_grad = pull_norm(normed_grad)
    resid_grad = output_grad.astype(jnp.float32) + back_resid
    branch_low = resid_grad.astype(jnp.bfloat16)
    crossproj_grad = left_product(mixed_two, branch_low)
    mixed_grad = right_product(branch_low, cross_proj).astype(jnp.bfloat16)
    query_back, key_back, value_back, unused_table = attend_backward(
        query_two, key_two, value_two, mixed_grad, lse_two, None
    )
    crossquery_grad = left_product(normed_two, query_back)
    crosskey_grad = left_product(encoder_states, key_back)
    crossvalue_grad = left_product(encoder_states, value_back)
    encoder_grad = right_product(key_back, cross_key) + right_product(value_back, cross_value)
    normed_grad = right_product(query_back, cross_query)
    norm_value, pull_norm = jax.vjp(rms_scale, after_self, gain_two.astype(jnp.float32))
    back_resid, gaincross_grad = pull_norm(normed_grad)
    resid_grad = resid_grad + back_resid
    branch_low = resid_grad.astype(jnp.bfloat16)
    selfproj_grad = left_product(mixed_one, branch_low)
    mixed_grad = right_product(branch_low, self_proj).astype(jnp.bfloat16)
    query_back, key_back, value_back, reltable_grad = attend_backward(
        query_one, key_one, value_one, mixed_grad, lse_one, context
    )
    selfquery_grad = left_product(normed_one, query_back)
    selfkey_grad = left_product(normed_one, key_back)
    selfvalue_grad = left_product(normed_one, value_back)
    normed_grad = (
        right_product(query_back, self_query)
        + right_product(key_back, self_key)
        + right_product(value_back, self_value)
    )
    norm_value, pull_norm = jax.vjp(rms_scale, resid_in, gain_one.astype(jnp.float32))
    back_resid, gainself_grad = pull_norm(normed_grad)
    hidden_grad = resid_grad + back_resid
    (
        owned_sq,
        owned_sk,
        owned_sv,
        owned_so,
        owned_cq,
        owned_ck,
        owned_cv,
        owned_co,
        owned_gate,
        owned_up,
        owned_down,
        owned_gself,
        owned_gcross,
        owned_gffn,
        owned_table,
    ) = (
        lax.psum_scatter(
            selfquery_grad.astype(jnp.bfloat16), "fsdp", scatter_dimension=0, tiled=True
        ).astype(jnp.float32),
        lax.psum_scatter(
            selfkey_grad.astype(jnp.bfloat16), "fsdp", scatter_dimension=0, tiled=True
        ).astype(jnp.float32),
        lax.psum_scatter(
            selfvalue_grad.astype(jnp.bfloat16), "fsdp", scatter_dimension=0, tiled=True
        ).astype(jnp.float32),
        lax.psum_scatter(
            selfproj_grad.astype(jnp.bfloat16), "fsdp", scatter_dimension=0, tiled=True
        ).astype(jnp.float32),
        lax.psum_scatter(
            crossquery_grad.astype(jnp.bfloat16), "fsdp", scatter_dimension=0, tiled=True
        ).astype(jnp.float32),
        lax.psum_scatter(
            crosskey_grad.astype(jnp.bfloat16), "fsdp", scatter_dimension=0, tiled=True
        ).astype(jnp.float32),
        lax.psum_scatter(
            crossvalue_grad.astype(jnp.bfloat16), "fsdp", scatter_dimension=0, tiled=True
        ).astype(jnp.float32),
        lax.psum_scatter(
            crossproj_grad.astype(jnp.bfloat16), "fsdp", scatter_dimension=0, tiled=True
        ).astype(jnp.float32),
        lax.psum_scatter(
            gateproj_grad.astype(jnp.bfloat16), "fsdp", scatter_dimension=0, tiled=True
        ).astype(jnp.float32),
        lax.psum_scatter(
            upproj_grad.astype(jnp.bfloat16), "fsdp", scatter_dimension=0, tiled=True
        ).astype(jnp.float32),
        lax.psum_scatter(
            downproj_grad.astype(jnp.bfloat16), "fsdp", scatter_dimension=0, tiled=True
        ).astype(jnp.float32),
        lax.psum_scatter(
            gainself_grad.astype(jnp.bfloat16), "fsdp", scatter_dimension=0, tiled=True
        ).astype(jnp.float32),
        lax.psum_scatter(
            gaincross_grad.astype(jnp.bfloat16), "fsdp", scatter_dimension=0, tiled=True
        ).astype(jnp.float32),
        lax.psum_scatter(
            gainffn_grad.astype(jnp.bfloat16), "fsdp", scatter_dimension=0, tiled=True
        ).astype(jnp.float32),
        lax.psum_scatter(
            reltable_grad.astype(jnp.bfloat16), "fsdp", scatter_dimension=0, tiled=True
        ).astype(jnp.float32),
    )
    results = lax.psum(
        (
            owned_sq,
            owned_sk,
            owned_sv,
            owned_so,
            owned_cq,
            owned_ck,
            owned_cv,
            owned_co,
            owned_gate,
            owned_up,
            owned_down,
            owned_gself,
            owned_gcross,
            owned_gffn,
            owned_table,
        ),
        "replica",
    )
    return (
        layer_out,
        hidden_grad,
        encoder_grad,
        results[0],
        results[1],
        results[2],
        results[3],
        results[4],
        results[5],
        results[6],
        results[7],
        results[8],
        results[9],
        results[10],
        results[11],
        results[12],
        results[13],
        results[14],
    )


def solution(mesh):
    placed = (
        P(("fsdp", "replica"), None),
        P(("fsdp", "replica"), None),
        P(("fsdp", "replica"), None),
        P(("fsdp", "replica"), None),
        P("fsdp", None),
        P("fsdp", None),
        P("fsdp", None),
        P("fsdp", None),
        P("fsdp", None),
        P("fsdp", None),
        P("fsdp", None),
        P("fsdp", None),
        P("fsdp", None),
        P("fsdp", None),
        P("fsdp", None),
        P("fsdp"),
        P("fsdp"),
        P("fsdp"),
        P("fsdp", None),
    )
    return jax.shard_map(
        on_device,
        mesh=mesh,
        in_specs=placed,
        out_specs=(
            P(("fsdp", "replica"), None),
            P(("fsdp", "replica"), None),
            P(("fsdp", "replica"), None),
            P("fsdp", None),
            P("fsdp", None),
            P("fsdp", None),
            P("fsdp", None),
            P("fsdp", None),
            P("fsdp", None),
            P("fsdp", None),
            P("fsdp", None),
            P("fsdp", None),
            P("fsdp", None),
            P("fsdp", None),
            P("fsdp"),
            P("fsdp"),
            P("fsdp"),
            P("fsdp", None),
        ),
        check_vma=False,
    )
```

profile of v0, /device:TPU:0, one launch (start us, length us, event | category | flops | bytes accessed | tf_op | source)
XLA Modules:
  0.0 1022.1 jit_solution(7677458020568450957)
XLA Ops:
  17.8 9.2 all-reduce.9
  33.2 9.2 fusion.1
  53.5 14.6 %all-gather.12.cloned.1.call-done = bf16[768,768]{1,0:T(8,128)(2,1)} async-done(((bf16[192,768]{1,0:T(8,128)(2,1)}), bf16[768,768]{1,0:T(8,128)(2,1)}) %all-gather.12.cloned.1.call-update) | async-done | bytes 1179664 | tf_op jit(solution)/shard_map/all_gather | solution.py:164
  72.5 14.5 %all-gather.20.cloned.1.call-done = bf16[768,768]{1,0:T(8,128)(2,1)} async-done(((bf16[192,768]{1,0:T(8,128)(2,1)}), bf16[768,768]{1,0:T(8,128)(2,1)}) %all-gather.20.cloned.1.call-update) | async-done | bytes 1179664 | tf_op jit(solution)/shard_map/all_gather | solution.py:168
  92.2 13.6 %all-gather.24.cloned.1.call-done = bf16[768,768]{1,0:T(8,128)(2,1)} async-done(((bf16[192,768]{1,0:T(8,128)(2,1)}), bf16[768,768]{1,0:T(8,128)(2,1)}) %all-gather.24.cloned.1.call-update) | async-done | bytes 1179664 | tf_op jit(solution)/shard_map/all_gather | solution.py:167
  111.1 15.1 %fusion.83 = (f32[12,512]{1,0:T(8,128)S(1)}, f32[12,512,512]{1,2,0:T(8,128)S(1)}) fusion(f32[512,512,12]{0,2,1:T(8,128)} %fusion.1, bf16[512,12,64]{0,2,1:T(8,128)(2,1)S(1)} %bitcast.136, bf16[512,12,64]{0,2,1:T(8,128)(2,1)S(1)} %bitcast.128, pred[512,512]{0,1:T(8,128)(4,1)S(1)} %copy-done.36), kind=kOutput, calls=%fused_computation.146 | convolution fusion | flops 412084224 | bytes 27025408 | tf_op jit(solution)/shard_map/qhd,khd->hqk/dot_general | solution.py:65
  167.0 25.9 %all-gather.30.cloned.1.call-done = bf16[768,2048]{1,0:T(8,128)(2,1)} async-done(((bf16[192,2048]{1,0:T(8,128)(2,1)}), bf16[768,2048]{1,0:T(8,128)(2,1)}) %all-gather.30.cloned.1.call-update) | async-done | bytes 3145744 | tf_op jit(solution)/shard_map/all_gather | solution.py:171
  198.8 24.0 %all-gather.28.cloned.1.call-done = bf16[768,2048]{1,0:T(8,128)(2,1)} async-done(((bf16[192,2048]{1,0:T(8,128)(2,1)}), bf16[768,2048]{1,0:T(8,128)(2,1)}) %all-gather.28.cloned.1.call-update) | async-done | bytes 3145744 | tf_op jit(solution)/shard_map/all_gather | solution.py:170
  228.8 24.1 %all-gather.32.cloned.1.call-done = bf16[2048,768]{1,0:T(8,128)(2,1)} async-done(((bf16[512,768]{1,0:T(8,128)(2,1)}), bf16[2048,768]{1,0:T(8,128)(2,1)}) %all-gather.32.cloned.1.call-update) | async-done | bytes 3145744 | tf_op jit(solution)/shard_map/all_gather | solution.py:172
  253.0 9.8 multiply_convert_fusion.2
  274.3 6.9 fusion.36
  286.3 7.9 multiply_reduce_fusion.1
  294.2 7.2 multiply_convert_fusion.1
  329.6 6.9 fusion.39
  346.1 7.3 multiply_convert_fusion
  391.5 7.6 fusion.47
  399.1 10.8 %all-reduce.8 = (bf16[768]{0:T(1024)(128)(2,1)S(1)}, bf16[768]{0:T(1024)(128)(2,1)S(1)}, bf16[768]{0:T(1024)(128)(2,1)S(1)}, bf16[32,12]{1,0:T(8,128)(2,1)S(1)}) all-reduce(bf16[768]{0:T(1024)(128)(2,1)S(1)} %get-tuple-element.94, bf16[768]{0:T(1024)(128)(2,1)S(1)} %get-tuple-element.92, ...), channel_id=13, replica_groups=mesh['fsdp'=4,'replica'=8] {'fsdp'}, use_global_device_ids=true, to_apply=%region_36.37.clone | all-reduce | flops 2688 | bytes 10752
  424.4 28.1 %reduce-scatter.20.cloned.1.call-done = bf16[192,768]{1,0:T(8,128)(2,1)} async-done(((bf16[768,768]{1,0:T(8,128)(2,1)}), bf16[192,768]{1,0:T(8,128)(2,1)}) %reduce-scatter.20.cloned.1.call-update) | async-done | bytes 294928 | tf_op jit(solution)/shard_map/reduce_scatter | solution.py:302
  452.5 28.1 %reduce-scatter.18.cloned.1.call-done = bf16[192,768]{1,0:T(8,128)(2,1)} async-done(((bf16[768,768]{1,0:T(8,128)(2,1)}), bf16[192,768]{1,0:T(8,128)(2,1)}) %reduce-scatter.18.cloned.1.call-update) | async-done | bytes 294928 | tf_op jit(solution)/shard_map/reduce_scatter | solution.py:299
  480.6 28.2 %reduce-scatter.16.cloned.1.call-done = bf16[192,768]{1,0:T(8,128)(2,1)} async-done(((bf16[768,768]{1,0:T(8,128)(2,1)}), bf16[192,768]{1,0:T(8,128)(2,1)}) %reduce-scatter.16.cloned.1.call-update) | async-done | bytes 294928 | tf_op jit(solution)/shard_map/reduce_scatter | solution.py:296
  508.8 40.3 %reduce-scatter.32.cloned.1.call-done = bf16[512,768]{1,0:T(8,128)(2,1)} async-done(((bf16[2048,768]{1,0:T(8,128)(2,1)}), bf16[512,768]{1,0:T(8,128)(2,1)}) %reduce-scatter.32.cloned.1.call-update) | async-done | bytes 786448 | tf_op jit(solution)/shard_map/reduce_scatter | solution.py:326
  549.1 40.5 %reduce-scatter.30.cloned.1.call-done = bf16[192,2048]{1,0:T(8,128)(2,1)} async-done(((bf16[768,2048]{1,0:T(8,128)(2,1)}), bf16[192,2048]{1,0:T(8,128)(2,1)}) %reduce-scatter.30.cloned.1.call-update) | async-done | bytes 786448 | tf_op jit(solution)/shard_map/reduce_scatter | solution.py:323
  589.5 40.5 %reduce-scatter.28.cloned.1.call-done = bf16[192,2048]{1,0:T(8,128)(2,1)} async-done(((bf16[768,2048]{1,0:T(8,128)(2,1)}), bf16[192,2048]{1,0:T(8,128)(2,1)}) %reduce-scatter.28.cloned.1.call-update) | async-done | bytes 786448 | tf_op jit(solution)/shard_map/reduce_scatter | solution.py:320
  630.0 382.7 %all-reduce.11 = (f32[192,768]{1,0:T(8,128)}, f32[192,768]{1,0:T(8,128)}, f32[192,768]{1,0:T(8,128)}, f32[192,768]{1,0:T(8,128)}, f32[192,768]{1,0:T(8,128)}, /*...) all-reduce(bf16[192,768]{1,0:T(8,128)(2,1)} %reduce-scatter.16.clon, ...), channel_id=1, replica_groups=mesh['fsdp'=4,'replica'=8] {'replica'}, use_global_device_ids=true, to_apply=%region_14.15 | all-reduce | flops 2359968 | bytes 14161152 | tf_op jit(solution)/shard_map/psum | solution.py:342
  (260 shorter events, 201.4 us)
Async XLA Ops:
  7.2 79.8 %copy-start = (bf16[512,768]{1,0:T(8,128)(2,1)S(1)}, bf16[512,768]{1,0:T(8,128)(2,1)}, u32[]{:S(2)}) copy-start(bf16[512,768]{1,0:T(8,128)(2,1)} %param.20) | copy-start | bytes 2359300
  7.2 35.2 %all-gather.14.cloned.1.call-start = ((), (), s32[]{:S(2)}) async-start(), calls=%async_computation.12 | async-start | bytes 1474560 | tf_op jit(solution)/shard_map/all_gather | solution.py:162
  7.9 41.1 %all-gather.16.cloned.1.call-start = ((), (), s32[]{:S(2)}) async-start(), calls=%async_computation.13 | async-start | bytes 1474560 | tf_op jit(solution)/shard_map/all_gather | solution.py:163
  8.7 59.4 %all-gather.12.cloned.1.call-start = ((), (), s32[]{:S(2)}) async-start(), calls=%async_computation.11 | async-start | bytes 1474560 | tf_op jit(solution)/shard_map/all_gather | solution.py:164
  9.4 77.6 %all-gather.20.cloned.1.call-start = ((), (), s32[]{:S(2)}) async-start(), calls=%async_computation.15 | async-start | bytes 1474560 | tf_op jit(solution)/shard_map/all_gather | solution.py:168
  10.0 95.9 %all-gather.24.cloned.1.call-start = ((), (), s32[]{:S(2)}) async-start(), calls=%async_computation.17 | async-start | bytes 1474560 | tf_op jit(solution)/shard_map/all_gather | solution.py:167
  10.6 123.7 %all-gather.18.cloned.1.call-start = ((), (), s32[]{:S(2)}) async-start(), calls=%async_computation.14 | async-start | bytes 1474560 | tf_op jit(solution)/shard_map/all_gather | solution.py:165
  11.2 132.6 %all-gather.22.cloned.1.call-start = ((), (), s32[]{:S(2)}) async-start(), calls=%async_computation.16 | async-start | bytes 1474560 | tf_op jit(solution)/shard_map/all_gather | solution.py:166
  11.9 150.9 %all-gather.26.cloned.1.call-start = ((), (), s32[]{:S(2)}) async-start(), calls=%async_computation.18 | async-start | bytes 1474560 | tf_op jit(solution)/shard_map/all_gather | solution.py:169
  12.7 180.2 %all-gather.30.cloned.1.call-start = ((), (), s32[]{:S(2)}) async-start(), calls=%async_computation.20 | async-start | bytes 3932160 | tf_op jit(solution)/shard_map/all_gather | solution.py:171
  13.5 209.4 %all-gather.28.cloned.1.call-start = ((), (), s32[]{:S(2)}) async-start(), calls=%async_computation.19 | async-start | bytes 3932160 | tf_op jit(solution)/shard_map/all_gather | solution.py:170
  14.1 238.9 %all-gather.32.cloned.1.call-start = ((), (), s32[]{:S(2)}) async-start(), calls=%async_computation.21 | async-start | bytes 3932160 | tf_op jit(solution)/shard_map/all_gather | solution.py:172
  14.8 406.2 %reduce-scatter.36.cloned.1.call-start = ((), (), s32[]{:S(2)}) async-start(), calls=%async_computation.32 | async-start | bytes 1474560
  165.7 98.9 %copy-start.9 = (f32[512,768]{1,0:T(8,128)}, f32[512,768]{1,0:T(8,128)S(1)}, u32[]{:S(2)}) copy-start(f32[512,768]{1,0:T(8,128)S(1)} %get-tuple-element.130) | copy-start | bytes 4718596
  286.2 135.9 %reduce-scatter.34.cloned.1.call-start = ((), (), s32[]{:S(2)}) async-start(), calls=%async_computation.31 | async-start | bytes 1474560
  309.1 114.3 %reduce-scatter.26.cloned.1.call-start = ((), (), s32[]{:S(2)}) async-start(), calls=%async_computation.27 | async-start | bytes 1474560 | tf_op jit(solution)/shard_map/reduce_scatter | solution.py:317
  312.1 111.2 %reduce-scatter.24.cloned.1.call-start = ((), (), s32[]{:S(2)}) async-start(), calls=%async_computation.26 | async-start | bytes 1474560 | tf_op jit(solution)/shard_map/reduce_scatter | solution.py:308
  319.3 105.1 %reduce-scatter.22.cloned.1.call-start = ((), (), s32[]{:S(2)}) async-start(), calls=%async_computation.25 | async-start | bytes 1474560 | tf_op jit(solution)/shard_map/reduce_scatter | solution.py:305
  325.2 127.3 %reduce-scatter.20.cloned.1.call-start = ((), (), s32[]{:S(2)}) async-start(), calls=%async_computation.24 | async-start | bytes 1474560 | tf_op jit(solution)/shard_map/reduce_scatter | solution.py:302
  339.5 141.1 %reduce-scatter.18.cloned.1.call-start = ((), (), s32[]{:S(2)}) async-start(), calls=%async_computation.23 | async-start | bytes 1474560 | tf_op jit(solution)/shard_map/reduce_scatter | solution.py:299
  359.0 149.8 %reduce-scatter.16.cloned.1.call-start = ((), (), s32[]{:S(2)}) async-start(), calls=%async_computation.22 | async-start | bytes 1474560 | tf_op jit(solution)/shard_map/reduce_scatter | solution.py:296
  365.9 183.2 %reduce-scatter.32.cloned.1.call-start = ((), (), s32[]{:S(2)}) async-start(), calls=%async_computation.30 | async-start | bytes 3932160 | tf_op jit(solution)/shard_map/reduce_scatter | solution.py:326
  371.1 218.4 %reduce-scatter.30.cloned.1.call-start = ((), (), s32[]{:S(2)}) async-start(), calls=%async_computation.29 | async-start | bytes 3932160 | tf_op jit(solution)/shard_map/reduce_scatter | solution.py:323
  377.4 252.6 %reduce-scatter.28.cloned.1.call-start = ((), (), s32[]{:S(2)}) async-start(), calls=%async_computation.28 | async-start | bytes 3932160 | tf_op jit(solution)/shard_map/reduce_scatter | solution.py:320
  (57 other events, 403.4 us)
Sparse Core Ops, SparseCore 0:
  9.6 20.4 all-gather.13
  31.6 17.4 all-gather.15
  50.6 17.4 all-gather.11
  69.5 17.4 all-gather.19
  88.4 17.4 all-gather.23
  107.3 17.4 all-gather.17
  126.3 17.4 all-gather.21
  145.3 17.4 all-gather.25
  164.4 28.4 all-gather.29
  194.3 28.4 all-gather.27
  224.4 28.4 all-gather.31
  286.4 25.6 reduce-scatter.35
  314.6 25.6 reduce-scatter.33
  342.7 25.6 reduce-scatter.25
  370.7 25.6 reduce-scatter.23
  398.8 25.6 reduce-scatter.21
  426.8 25.6 reduce-scatter.19
  454.9 25.6 reduce-scatter.17
  483.1 25.6 reduce-scatter.15
  511.2 37.8 reduce-scatter.31
  551.6 37.8 reduce-scatter.29
  592.1 37.8 reduce-scatter.27
where the time goes:
time: 1030 us; the launch traced here: 1020 us
  blocking collectives  408 us (40%)
  waiting for transfers between devices  344 us (33%)
  matrix products  184 us (18%)
  local copies, waits for them, and re-layouts  41.8 us (4%)
  other arithmetic  25.3 us (2%)
  between operations  17.8 us (2%)
    psum x1, blocking collectives, on_device(): lax.psum((owned_sq, owned_sk, owned_sv, owned_so, owned_cq, owned_ck, own...  383 us
    reduce_scatter x1, waiting for transfers between devices, on_device(): lax.psum_scatter(upproj_grad.astype(jnp.bfloat16), 'fsdp', scatter_dimens...  40.5 us
    reduce_scatter x1, waiting for transfers between devices, on_device(): lax.psum_scatter(gateproj_grad.astype(jnp.bfloat16), 'fsdp', scatter_dime...  40.5 us
    reduce_scatter x1, waiting for transfers between devices, on_device(): lax.psum_scatter(downproj_grad.astype(jnp.bfloat16), 'fsdp', scatter_dime...  40.3 us
    dot_general x11, matrix products, product(): return jnp.dot(left, right, preferred_element_type=jnp.float32)  37.1 us
    dot_general x11, matrix products, right_product(): lax.dot_general(left, right, (((1,), (1,)), ((), ())), preferred_element_...  32.7 us
    dot_general x11, matrix products, left_product(): lax.dot_general(left, right, (((0,), (0,)), ((), ())), preferred_element_...  31.8 us
    reduce_scatter x1, waiting for transfers between devices, on_device(): lax.psum_scatter(selfquery_grad.astype(jnp.bfloat16), 'fsdp', scatter_dim...  28.2 us
  transfers between devices with their start and end apart: 22, of which 16 were waited for; matrix products, arithmetic and copies ran while one was open for 20% of the time, Pallas kernels for 0%

commit v1 on v0

v1 whole, which is shorter than its diff:
```python
import jax
import jax.numpy as jnp
from jax import lax
from jax.sharding import PartitionSpec as P

HEADS = 12
HEAD_DIM = 64
BUCKETS = 32
QBLOCK = 512


EPS = 1e-06
NEG = -1000000000.0
EDGES = (1, 2, 3, 4, 5, 6, 7, 8, 12, 16, 23, 32, 46, 64, 91)


def rms_scale(hidden, gain):
    return hidden * lax.rsqrt(jnp.mean(hidden * hidden, axis=-1, keepdims=True) + EPS) * gain


def gated(gate, upper):
    return jax.nn.gelu(gate, approximate=True) * upper


def product(left, right):
    return jnp.dot(left, right, preferred_element_type=jnp.float32)


def left_product(left, right):
    return lax.dot_general(
        left, right, (((0,), (0,)), ((), ())), preferred_element_type=jnp.float32
    )


def right_product(left, right):
    return lax.dot_general(
        left, right, (((1,), (1,)), ((), ())), preferred_element_type=jnp.float32
    )


def split_heads(matrix):
    return matrix.reshape(matrix.shape[0], HEADS, HEAD_DIM)


def block_terms(context, block_rows, key_count):
    if context is None:
        return (None, None, None)
    rel_table, piece_ids = context
    query_pos = jnp.arange(block_rows, dtype=jnp.int32)
    key_pos = jnp.arange(key_count, dtype=jnp.int32)
    relative = key_pos[None, :] - query_pos[:, None]
    distance = jnp.abs(relative)
    bucket = 16 * (relative > 0).astype(jnp.int32)
    for edge_len in EDGES:
        bucket = bucket + (distance >= edge_len).astype(jnp.int32)
    onehot = (bucket[:, :, None] == jnp.arange(BUCKETS, dtype=jnp.int32)[None, None, :]).astype(
        jnp.bfloat16
    )
    bias_block = jnp.einsum("qkb,bh->hqk", onehot, rel_table, preferred_element_type=jnp.float32)
    allowed = (key_pos[None, :] <= query_pos[:, None]) | (piece_ids[None, :] == piece_ids[:, None])
    return (onehot, bias_block, allowed)


def block_scores(query_block, key_heads, bias_block, allowed):
    scores = jnp.einsum("qhd,khd->hqk", query_block, key_heads, preferred_element_type=jnp.float32)
    if bias_block is not None:
        scores = jnp.where(allowed[None], scores + bias_block, NEG)
    return scores


def attend_forward(queries, key_rows, value_rows, context):
    key_heads = split_heads(key_rows)
    value_heads = split_heads(value_rows)
    query_block = split_heads(queries)
    onehot, bias_block, allowed = block_terms(context, QBLOCK, key_rows.shape[0])
    scores = block_scores(query_block, key_heads, bias_block, allowed)
    row_max = jnp.max(scores, axis=-1, keepdims=True)
    raised = jnp.exp(scores - row_max)
    row_sum = jnp.sum(raised, axis=-1, keepdims=True)
    prob_low = (raised / row_sum).astype(jnp.bfloat16)
    mixed_block = jnp.einsum(
        "hqk,khd->qhd", prob_low, value_heads, preferred_element_type=jnp.float32
    )
    mixed_parts = mixed_block.reshape(QBLOCK, HEADS * HEAD_DIM).astype(jnp.bfloat16)
    lse_parts = row_max + jnp.log(row_sum)
    return (mixed_parts, lse_parts)


def attend_backward(queries, key_rows, value_rows, grad_mixed, lse_rows, context):
    key_count = key_rows.shape[0]
    key_heads = split_heads(key_rows)
    value_heads = split_heads(value_rows)
    table_grad = jnp.zeros((BUCKETS, HEADS), jnp.float32)
    query_block = split_heads(queries)
    grad_block = split_heads(grad_mixed)
    onehot, bias_block, allowed = block_terms(context, QBLOCK, key_count)
    scores = block_scores(query_block, key_heads, bias_block, allowed)
    probs = jnp.exp(scores - lse_rows)
    prob_low = probs.astype(jnp.bfloat16)
    grad_probs = jnp.einsum(
        "qhd,khd->hqk", grad_block, value_heads, preferred_element_type=jnp.float32
    )
    inner_sum = jnp.sum(probs * grad_probs, axis=-1, keepdims=True)
    grad_scores = (probs * (grad_probs - inner_sum)).astype(jnp.bfloat16)
    query_grad = jnp.einsum(
        "hqk,khd->qhd", grad_scores, key_heads, preferred_element_type=jnp.float32
    )
    query_parts = query_grad.reshape(QBLOCK, HEADS * HEAD_DIM).astype(jnp.bfloat16)
    key_grad = jnp.einsum(
        "hqk,qhd->khd", grad_scores, query_block, preferred_element_type=jnp.float32
    )
    value_grad = jnp.einsum(
        "hqk,qhd->khd", prob_low, grad_block, preferred_element_type=jnp.float32
    )
    if onehot is not None:
        table_grad = jnp.einsum(
            "hqk,qkb->bh", grad_scores, onehot, preferred_element_type=jnp.float32
        )
    key_low = key_grad.reshape(key_count, HEADS * HEAD_DIM).astype(jnp.bfloat16)
    value_low = value_grad.reshape(key_count, HEADS * HEAD_DIM).astype(jnp.bfloat16)
    return (query_parts, key_low, value_low, table_grad)


def make_on_device(fsdp_size, replica_size):
    def on_device(
        hidden_in,
        encoder_states,
        output_grad,
        piece_starts,
        selfquery,
        selfkey,
        selfvalue,
        selfproj,
        crossquery,
        crosskey,
        crossvalue,
        crossproj,
        gateproj,
        upproj,
        downproj,
        gainself,
        gaincross,
        gainffn,
        reltable,
    ):
        shard_rows, width = selfquery.shape
        ff_width = gateproj.shape[1]
        table_rows = reltable.shape[0]
        self_packed = jnp.concatenate([selfquery, selfkey, selfvalue], axis=1)
        small_packed = jnp.concatenate(
            [gainself, gaincross, gainffn, reltable.reshape(-1)]
        )
        mid_packed = jnp.concatenate(
            [selfproj, crossquery, crosskey, crossvalue, crossproj], axis=1
        )
        ffn_packed = jnp.concatenate(
            [gateproj, upproj, downproj.reshape(shard_rows, -1)], axis=1
        )
        self_full = lax.all_gather(self_packed, "fsdp", axis=0, tiled=True)
        small_full = lax.all_gather(small_packed, "fsdp", axis=0, tiled=False)
        mid_full = lax.all_gather(mid_packed, "fsdp", axis=0, tiled=True)
        ffn_full = lax.all_gather(ffn_packed, "fsdp", axis=0, tiled=True)

        gain_one = small_full[:, 0:shard_rows].reshape(-1)
        gain_two = small_full[:, shard_rows : 2 * shard_rows].reshape(-1)
        gain_three = small_full[:, 2 * shard_rows : 3 * shard_rows].reshape(-1)
        table_full = small_full[:, 3 * shard_rows :].reshape(-1, HEADS)
        self_proj = mid_full[:, 0:width]
        cross_query = mid_full[:, width : 2 * width]
        cross_kv = mid_full[:, 2 * width : 4 * width]
        cross_key = cross_kv[:, :width]
        cross_value = cross_kv[:, width:]
        cross_proj = mid_full[:, 4 * width : 5 * width]
        gate_up = ffn_full[:, : 2 * ff_width]
        down_full = (
            ffn_full[:, 2 * ff_width :]
            .reshape(fsdp_size, shard_rows, ff_width)
            .reshape(ff_width, width)
        )

        length = hidden_in.shape[0]
        position = jnp.arange(length, dtype=jnp.int32)
        piece_ids = (
            jnp.sum((piece_starts[0][None, :] <= position[:, None]).astype(jnp.int32), axis=1) - 1
        )
        context = (table_full, piece_ids)
        resid_in = hidden_in.astype(jnp.float32)
        normed_one = rms_scale(resid_in, gain_one.astype(jnp.float32)).astype(jnp.bfloat16)
        qkv_one = product(normed_one, self_full).astype(jnp.bfloat16)
        query_one = qkv_one[:, :width]
        key_one = qkv_one[:, width : 2 * width]
        value_one = qkv_one[:, 2 * width :]
        mixed_one, lse_one = attend_forward(query_one, key_one, value_one, context)
        after_self = resid_in + product(mixed_one, self_proj)
        normed_two = rms_scale(after_self, gain_two.astype(jnp.float32)).astype(jnp.bfloat16)
        query_two = product(normed_two, cross_query).astype(jnp.bfloat16)
        kv_two = product(encoder_states, cross_kv).astype(jnp.bfloat16)
        key_two = kv_two[:, :width]
        value_two = kv_two[:, width:]
        mixed_two, lse_two = attend_forward(query_two, key_two, value_two, None)
        after_cross = after_self + product(mixed_two, cross_proj)
        normed_three = rms_scale(after_cross, gain_three.astype(jnp.float32)).astype(jnp.bfloat16)
        gate_upper = product(normed_three, gate_up)
        gate_pre = gate_upper[:, :ff_width]
        upper_pre = gate_upper[:, ff_width:]
        inner = gated(gate_pre, upper_pre).astype(jnp.bfloat16)
        layer_out = (after_cross + product(inner, down_full)).astype(jnp.bfloat16)

        def reduce_rows(packed):
            owned = lax.psum_scatter(
                packed.astype(jnp.bfloat16), ("fsdp", "replica"), scatter_dimension=0, tiled=True
            )
            return lax.all_gather(owned, "replica", axis=0, tiled=True)

        downproj_grad = left_product(inner, output_grad)
        inner_grad = right_product(output_grad, down_full)
        gated_value, pull_gate = jax.vjp(gated, gate_pre, upper_pre)
        gate_grad, upper_grad = pull_gate(inner_grad)
        gate_upper_low = jnp.concatenate(
            [gate_grad.astype(jnp.bfloat16), upper_grad.astype(jnp.bfloat16)], axis=1
        )
        gate_up_grad = left_product(normed_three, gate_upper_low)
        ffn_owned = reduce_rows(
            jnp.concatenate([gate_up_grad, downproj_grad.reshape(width, ff_width)], axis=1)
        )
        normed_grad = right_product(gate_upper_low, gate_up)
        norm_value, pull_norm = jax.vjp(rms_scale, after_cross, gain_three.astype(jnp.float32))
        back_resid, gainffn_grad = pull_norm(normed_grad)
        resid_grad = output_grad.astype(jnp.float32) + back_resid
        branch_low = resid_grad.astype(jnp.bfloat16)
        crossproj_grad = left_product(mixed_two, branch_low)
        mixed_grad = right_product(branch_low, cross_proj).astype(jnp.bfloat16)
        query_back, key_back, value_back, unused_table = attend_backward(
            query_two, key_two, value_two, mixed_grad, lse_two, None
        )
        crossquery_grad = left_product(normed_two, query_back)
        kv_back = jnp.concatenate([key_back, value_back], axis=1)
        crosskv_grad = left_product(encoder_states, kv_back)
        cross_owned = reduce_rows(
            jnp.concatenate([crossproj_grad, crossquery_grad, crosskv_grad], axis=1)
        )
        encoder_grad = right_product(kv_back, cross_kv)
        normed_grad = right_product(query_back, cross_query)
        norm_value, pull_norm = jax.vjp(rms_scale, after_self, gain_two.astype(jnp.float32))
        back_resid, gaincross_grad = pull_norm(normed_grad)
        resid_grad = resid_grad + back_resid
        branch_low = resid_grad.astype(jnp.bfloat16)
        selfproj_grad = left_product(mixed_one, branch_low)
        mixed_grad = right_product(branch_low, self_proj).astype(jnp.bfloat16)
        query_back, key_back, value_back, reltable_grad = attend_backward(
            query_one, key_one, value_one, mixed_grad, lse_one, context
        )
        qkv_back = jnp.concatenate([query_back, key_back, value_back], axis=1)
        selfqkv_grad = left_product(normed_one, qkv_back)
        self_owned = reduce_rows(jnp.concatenate([selfproj_grad, selfqkv_grad], axis=1))
        normed_grad = right_product(qkv_back, self_full)
        norm_value, pull_norm = jax.vjp(rms_scale, resid_in, gain_one.astype(jnp.float32))
        back_resid, gainself_grad = pull_norm(normed_grad)
        hidden_grad = resid_grad + back_resid

        small_sum = lax.psum(
            jnp.concatenate(
                [gainself_grad, gaincross_grad, gainffn_grad, reltable_grad.reshape(-1)]
            ),
            ("fsdp", "replica"),
        )
        me = lax.axis_index("fsdp")
        gain_block = lambda i: lax.dynamic_slice_in_dim(
            small_sum, i * width + me * shard_rows, shard_rows
        )
        table_block = lax.dynamic_slice_in_dim(
            small_sum[3 * width :].reshape(-1, HEADS), me * table_rows, table_rows
        )

        as_f32 = lambda v: v.astype(jnp.float32)
        return (
            layer_out,
            hidden_grad,
            encoder_grad,
            as_f32(self_owned[:, width : 2 * width]),
            as_f32(self_owned[:, 2 * width : 3 * width]),
            as_f32(self_owned[:, 3 * width : 4 * width]),
            as_f32(self_owned[:, 0:width]),
            as_f32(cross_owned[:, width : 2 * width]),
            as_f32(cross_owned[:, 2 * width : 3 * width]),
            as_f32(cross_owned[:, 3 * width : 4 * width]),
            as_f32(cross_owned[:, 0:width]),
            as_f32(ffn_owned[:, 0:ff_width]),
            as_f32(ffn_owned[:, ff_width : 2 * ff_width]),
            as_f32(ffn_owned[:, 2 * ff_width :].reshape(-1, width)),
            gain_block(0),
            gain_block(1),
            gain_block(2),
            table_block,
        )

    return on_device


def solution(mesh):
    placed = (
        P(("fsdp", "replica"), None),
        P(("fsdp", "replica"), None),
        P(("fsdp", "replica"), None),
        P(("fsdp", "replica"), None),
        P("fsdp", None),
        P("fsdp", None),
        P("fsdp", None),
        P("fsdp", None),
        P("fsdp", None),
        P("fsdp", None),
        P("fsdp", None),
        P("fsdp", None),
        P("fsdp", None),
        P("fsdp", None),
        P("fsdp", None),
        P("fsdp"),
        P("fsdp"),
        P("fsdp"),
        P("fsdp", None),
    )
    return jax.shard_map(
        make_on_device(mesh.shape["fsdp"], mesh.shape["replica"]),
        mesh=mesh,
        in_specs=placed,
        out_specs=(
            P(("fsdp", "replica"), None),
            P(("fsdp", "replica"), None),
            P(("fsdp", "replica"), None),
            P("fsdp", None),
            P("fsdp", None),
            P("fsdp", None),
            P("fsdp", None),
            P("fsdp", None),
            P("fsdp", None),
            P("fsdp", None),
            P("fsdp", None),
            P("fsdp", None),
            P("fsdp", None),
            P("fsdp", None),
            P("fsdp"),
            P("fsdp"),
            P("fsdp"),
            P("fsdp", None),
        ),
        check_vma=False,
    )
```

time: 1030 us -> 761 us (0.74)
  blocking collectives: 408 us -> 50.2 us
  local copies, waits for them, and re-layouts: 41.8 us -> 123 us
  matrix products: 184 us -> 149 us
  other arithmetic: 25.3 us -> 56.9 us
  waiting for transfers between devices: 344 us -> 357 us
    psum x1, blocking collectives: 383 us -> 40.9 us  [on_device(): lax.psum(jnp.concatenate([gainself_grad, gaincross_grad, gainffn_grad, re...]
    reduce_scatter x9 -> x3, waiting for transfers between devices: 207 us -> 292 us  [reduce_rows(): lax.psum_scatter(packed.astype(jnp.bfloat16), ('fsdp', 'replica'), scatte...]
    all_gather x11 -> x6, waiting for transfers between devices: 131 us -> 64.7 us  [the longest x3 64.6 us: reduce_rows(): return lax.all_gather(owned, 'replica', axis=0, tiled=True)]
    eq x0 -> x1, local copies, waits for them, and re-layouts: none -> 45.9 us  [block_terms(): bucket[:, :, None] == jnp.arange(BUCKETS, dtype=jnp.int32)[None, None, :]]
    dot_general x0 -> x1, local copies, waits for them, and re-layouts: none -> 18 us  [block_terms(): jnp.einsum('qkb,bh->hqk', onehot, rel_table, preferred_element_type=jnp.f...]
    concatenate x0 -> x7, other arithmetic: none -> 14.4 us  [the longest x1 4.21 us: on_device(): jnp.concatenate([gate_up_grad, downproj_grad.reshape(width, ff_width)], a...]
    dot_general x11 -> x7, matrix products: 31.8 us -> 19.7 us  [left_product(): lax.dot_general(left, right, (((0,), (0,)), ((), ())), preferred_element_...]
    unnamed x2 -> x1, blocking collectives: 20 us -> 9.28 us
  transfers between devices with their start and end apart: 22 -> 9, of which waited for: 16 -> 5; matrix products, arithmetic and copies ran while one was open for 20% -> 31% of each run, Pallas kernels for 0% -> 0%
where the time goes in v1:
time: 761 us; the launch traced here: 753 us
  waiting for transfers between devices  357 us (47%)
  matrix products  149 us (20%)
  local copies, waits for them, and re-layouts  123 us (16%)
  other arithmetic  56.9 us (7%)
  blocking collectives  50.2 us (7%)
  between operations  15.8 us (2%)
    reduce_scatter x3, waiting for transfers between devices, reduce_rows(): lax.psum_scatter(packed.astype(jnp.bfloat16), ('fsdp', 'replica'), scatte...  292 us
    all_gather x3, waiting for transfers between devices, reduce_rows(): return lax.all_gather(owned, 'replica', axis=0, tiled=True)  64.6 us
    eq x1, local copies, waits for them, and re-layouts, block_terms(): bucket[:, :, None] == jnp.arange(BUCKETS, dtype=jnp.int32)[None, None, :]  45.9 us
    psum x1, blocking collectives, on_device(): lax.psum(jnp.concatenate([gainself_grad, gaincross_grad, gainffn_grad, re...  40.9 us
    dot_general x7, matrix products, right_product(): lax.dot_general(left, right, (((1,), (1,)), ((), ())), preferred_element_...  31.5 us
    dot_general x7, matrix products, product(): return jnp.dot(left, right, preferred_element_type=jnp.float32)  29.6 us
    dot_general x2, matrix products, attend_backward(): jnp.einsum('qhd,khd->hqk', grad_block, value_heads, preferred_element_typ...  21.8 us
    unnamed x148, local copies, waits for them, and re-layouts  21.7 us
  transfers between devices with their start and end apart: 9, of which 5 were waited for; matrix products, arithmetic and copies ran while one was open for 31% of the time, Pallas kernels for 0%

profile of v1, /device:TPU:0, one launch (start us, length us, event | category | flops | bytes accessed | tf_op | source)
XLA Modules:
  0.0 752.9 jit_solution(3771571763767273229)
XLA Ops:
  21.4 9.3 %all-reduce = bf16[2688]{0:T(1024)(128)(2,1)S(1)} all-reduce(bf16[2688]{0:T(1024)(128)(2,1)S(1)} %dynamic-update-slice), channel_id=2, replica_groups=mesh['fsdp'=4,'replica'=8] {'fsdp'}, use_global_device_ids=true, to_apply=%add | all-reduce | flops 2688 | bytes 10752
  31.9 8.7 %iota_compare_fusion = pred[512,512,32]{0,2,1:T(32,128)(4,1)} fusion(s32[512,512]{0,1:T(8,128)S(1)} %convert_add_fusion.1), kind=kLoop, calls=%fused_computation | loop fusion | flops 8388608 | bytes 9437184 | tf_op jit(solution)/shard_map/eq | solution.py:56
  40.5 45.9 %copy.117 = pred[512,512,32]{1,2,0:T(32,128)(4,1)S(1)} copy(pred[512,512,32]{0,2,1:T(32,128)(4,1)} %iota_compare_fusion) | data formatting | bytes 16777216 | tf_op jit(solution)/shard_map/eq | solution.py:56
  86.5 7.7 %fusion.83 = f32[12,512,512]{2,0,1:T(8,128)} fusion(pred[512,512,32]{1,2,0:T(32,128)(4,1)S(1)} %copy.117, bf16[32,12]{1,0:T(8,128)(2,1)S(1)} %reshape.325), kind=kOutput, calls=%fused_computation.155 | convolution fusion | flops 201326592 | bytes 20972288 | tf_op jit(solution)/shard_map/qkb,bh->hqk/dot_general | solution.py:59
  94.2 18.0 %copy.118 = f32[12,512,512]{1,2,0:T(8,128)} copy(f32[12,512,512]{2,0,1:T(8,128)} %fusion.83) | data formatting | bytes 25165824 | tf_op jit(solution)/shard_map/qkb,bh->hqk/dot_general | solution.py:59
  120.5 6.7 fusion.97
  165.4 6.6 reshape_reshape.3
  172.0 10.2 %fusion.16 = f32[512,4096]{1,0:T(8,128)} fusion(bf16[768,6144]{1,0:T(8,128)(2,1)} %all-gather.12.cloned.1.call-done, f32[512,768]{1,0:T(8,128)} %get-tuple-element.92, f32[768]{0:T(1024)S(1)} %reshape.337, f32[512]{0:T(512)S(1)} %fusion.87), kind=kOutput, calls=%fused_computation.30 | convolution fusion | flops 3222405120 | bytes 16258048 | tf_op jit(solution)/shard_map/dot_general | solution.py:26
  182.3 8.3 %fusion.24 = (bf16[512,2048]{1,0:T(8,128)(2,1)S(1)}, bf16[512,2048]{1,0:T(8,128)(2,1)S(1)}, bf16[512,2048]{1,0:T(8,128)(2,1)}) fusion(f32[512,4096]{1,0:T(8,128)} %fusion.16, bf16[2048,768]{1,0:T(8,128)(2,1)S(1)} %copy-done.28, bf16[512,768]{1,0:T(8,128)(2,1)S(1)} %copy-done.42), kind=kOutput, calls=%fused_computation.42 | convolution fusion | flops 1637875712 | bytes 18612224 | tf_op jit(solution)/shard_map/dot_general | solution.py:36
  202.7 7.9 %fusion.40 = bf16[12,64,512]{2,1,0:T(8,128)(2,1)} fusion(bf16[512,12,64]{0,2,1:T(8,128)(2,1)} %bitcast.98, f32[12,512,512]{1,2,0:T(8,128)} %copy-done.2, f32[12,512]{1,0:T(8,128)S(1)} %log_add_fusion.1), kind=kOutput, calls=%fused_computation.93 | convolution fusion | flops 409337856 | bytes 14180352 | tf_op jit(solution)/shard_map/hqk,qhd->khd/dot_general | solution.py:112
  210.6 9.0 %multiply_reduce_fusion.1 = (f32[12,512]{1,0:T(8,128)S(1)}, f32[12,512,512]{1,2,0:T(8,128)}) fusion(f32[12,512,512]{1,2,0:T(8,128)} %copy-done.2, f32[12,512]{1,0:T(8,128)S(1)} %log_add_fusion.1, bf16[512,12,64]{0,2,1:T(8,128)(2,1)S(1)} %bitcast.99, bf16[512,12,64]{0,2,1:T(8,128)(2,1)S(1)} %bitcast.109), kind=kOutput, calls=%fused_computation.5 | convolution fusion | flops 412084224 | bytes 26787840 | tf_op jit(solution)/shard_map/qhd,khd->hqk/dot_general | solution.py:100
  219.5 7.1 multiply_convert_fusion.1
  235.1 6.6 copy.148
  256.5 12.8 %multiply_reduce_fusion = (f32[12,512]{1,0:T(8,128)S(1)}, f32[12,512,512]{1,2,0:T(8,128)}) fusion(f32[12,512,512]{1,2,0:T(8,128)} %copy-done.1, f32[12,512]{1,0:T(8,128)S(1)} %log_add_fusion, bf16[512,12,64]{0,2,1:T(8,128)(2,1)} %bitcast.96, bf16[512,12,64]{0,2,1:T(8,128)(2,1)} %bitcast.107), kind=kOutput, calls=%fused_computation.2 | convolution fusion | flops 412084224 | bytes 26787840 | tf_op jit(solution)/shard_map/qhd,khd->hqk/dot_general | solution.py:100
  269.3 7.1 multiply_convert_fusion
  293.9 6.6 reshape.332
  300.5 6.4 convolution_convert_fusion
  311.2 38.8 %reduce-scatter.10.cloned.1.call-done = bf16[24,3072]{1,0:T(8,128)(2,1)} async-done(((bf16[768,3072]{1,0:T(8,128)(2,1)}), bf16[24,3072]{1,0:T(8,128)(2,1)}) %reduce-scatter.10.cloned.1.call-update) | async-done | bytes 147472 | tf_op jit(solution)/shard_map/reduce_scatter | solution.py:210
  350.1 111.8 %reduce-scatter.6.cloned.1.call-done = bf16[24,3072]{1,0:T(8,128)(2,1)} async-done(((bf16[768,3072]{1,0:T(8,128)(2,1)}), bf16[24,3072]{1,0:T(8,128)(2,1)}) %reduce-scatter.6.cloned.1.call-update) | async-done | bytes 147472 | tf_op jit(solution)/shard_map/reduce_scatter | solution.py:210
  462.0 141.3 %reduce-scatter.8.cloned.1.call-done = bf16[24,6144]{1,0:T(8,128)(2,1)} async-done(((bf16[768,6144]{1,0:T(8,128)(2,1)}), bf16[24,6144]{1,0:T(8,128)(2,1)}) %reduce-scatter.8.cloned.1.call-update) | async-done | bytes 294928 | tf_op jit(solution)/shard_map/reduce_scatter | solution.py:210
  603.4 8.5 %fusion.48 = f32[32,12]{1,0:T(8,128)S(1)} fusion(bf16[12,512,512]{1,2,0:T(8,128)(2,1)} %copy-done.3, s32[512,512]{0,1:T(8,128)S(1)} %copy-done.22), kind=kOutput, calls=%fused_computation.101 | convolution fusion | flops 209715200 | bytes 7341568 | tf_op jit(solution)/shard_map/hqk,qkb->bh/dot_general | solution.py:116
  618.4 40.9 %psum.7 = f32[2688]{0:T(1024)S(1)} all-reduce(f32[2688]{0:T(1024)S(1)} %pad_maximum_fusion.14), channel_id=1, replica_groups=mesh['fsdp'=4,'replica'=8] {'fsdp','replica'}, use_global_device_ids=true, to_apply=%region_19.20 | all-reduce | flops 2688 | bytes 21504 | tf_op jit(solution)/shard_map/psum | solution.py:261
  673.4 14.6 %all-gather.14.cloned.1.call-done = bf16[192,3072]{1,0:T(8,128)(2,1)} async-done(((bf16[24,3072]{1,0:T(8,128)(2,1)}), bf16[192,3072]{1,0:T(8,128)(2,1)}) %all-gather.14.cloned.1.call-update) | async-done | bytes 1179664 | tf_op jit(solution)/shard_map/all_gather | solution.py:213
  690.7 50.1 %all-gather.18.cloned.1.call-done = bf16[192,6144]{1,0:T(8,128)(2,1)} async-done(((bf16[24,6144]{1,0:T(8,128)(2,1)}), bf16[192,6144]{1,0:T(8,128)(2,1)}) %all-gather.18.cloned.1.call-update) | async-done | bytes 2359312 | tf_op jit(solution)/shard_map/all_gather | solution.py:213
  (252 shorter events, 146.2 us)
Async XLA Ops:
  7.2 136.4 %copy-start = (bf16[512,768]{1,0:T(8,128)(2,1)S(1)}, bf16[512,768]{1,0:T(8,128)(2,1)}, u32[]{:S(2)}) copy-start(bf16[512,768]{1,0:T(8,128)(2,1)} %param.20) | copy-start | bytes 2359300
  7.2 105.6 %all-gather.8.cloned.1.call-start = ((), (), s32[]{:S(2)}) async-start(), calls=%async_computation.3 | async-start | bytes 4423680 | tf_op jit(solution)/shard_map/all_gather | solution.py:159
  9.5 125.5 %all-gather.10.cloned.1.call-start = ((), (), s32[]{:S(2)}) async-start(), calls=%async_computation.4 | async-start | bytes 7372800 | tf_op jit(solution)/shard_map/all_gather | solution.py:161
  14.7 146.7 %all-gather.12.cloned.1.call-start = ((), (), s32[]{:S(2)}) async-start(), calls=%async_computation.5 | async-start | bytes 11796480 | tf_op jit(solution)/shard_map/all_gather | solution.py:162
  19.7 330.3 %reduce-scatter.10.cloned.1.call-start = ((), (), s32[]{:S(2)}) async-start(), calls=%async_computation.11 | async-start | bytes 4866048 | tf_op jit(solution)/shard_map/reduce_scatter | solution.py:210
  31.1 81.7 %copy-start.50 = (f32[768]{0:T(1024)}, f32[768]{0:T(1024)S(1)}, u32[]{:S(2)}) copy-start(f32[768]{0:T(1024)S(1)} %reshape.335) | copy-start | bytes 9220
  94.2 18.0 %copy-start.55 = (s32[1,3]{1,0:T(1,128)S(1)}, s32[1,3]{1,0:T(1,128)}, u32[]{:S(2)}) copy-start(s32[1,3]{1,0:T(1,128)} %param.22) | copy-start | bytes 40
  94.2 18.1 %copy-start.30 = (bf16[512,768]{1,0:T(8,128)(2,1)S(1)}, bf16[512,768]{1,0:T(8,128)(2,1)}, u32[]{:S(2)}) copy-start(bf16[512,768]{1,0:T(8,128)(2,1)} %param.19) | copy-start | bytes 2359300
  137.6 104.2 %copy-start.6 = (f32[512,768]{1,0:T(8,128)}, f32[512,768]{1,0:T(8,128)S(1)}, u32[]{:S(2)}) copy-start(f32[512,768]{1,0:T(8,128)S(1)} %get-tuple-element.88) | copy-start | bytes 4718596
  172.0 10.2 %copy-start.42 = (bf16[512,768]{1,0:T(8,128)(2,1)S(1)}, bf16[512,768]{1,0:T(8,128)(2,1)}, u32[]{:S(2)}) copy-start(bf16[512,768]{1,0:T(8,128)(2,1)} %param.21) | copy-start | bytes 2359300
  172.0 18.6 %slice-start.6 = ((s8[9437184]{0:T(1024)(128)(4,1)}), s8[4194304]{0:T(1024)(128)(4,1)S(1)}, s32[]{:S(2)}) async-start(s8[9437184]{0:T(1024)(128)(4,1)} %bitcast.114), calls=%async_computation.18 | async-start | bytes 8388608
  202.6 16.9 %slice-start.3 = ((s8[12582912]{0:T(1024)(128)(4,1)}), s8[4194304]{0:T(1024)(128)(4,1)S(1)}, s32[]{:S(2)}) async-start(s8[12582912]{0:T(1024)(128)(4,1)} %bitcast.90), calls=%async_computation.15 | async-start | bytes 8388608
  202.7 16.9 %slice-start.4 = ((s8[12582912]{0:T(1024)(128)(4,1)}), s8[4194304]{0:T(1024)(128)(4,1)S(1)}, s32[]{:S(2)}) async-start(s8[12582912]{0:T(1024)(128)(4,1)} %bitcast.90), calls=%async_computation.16 | async-start | bytes 8388608
  241.8 220.1 %reduce-scatter.6.cloned.1.call-start = ((), (), s32[]{:S(2)}) async-start(), calls=%async_computation.6 | async-start | bytes 4866048 | tf_op jit(solution)/shard_map/reduce_scatter | solution.py:210
  256.5 12.8 %slice-start = ((s8[12582912]{0:T(1024)(128)(4,1)}), s8[4194304]{0:T(1024)(128)(4,1)S(1)}, s32[]{:S(2)}) async-start(s8[12582912]{0:T(1024)(128)(4,1)} %bitcast.88), calls=%async_computation.12 | async-start | bytes 8388608
  256.5 12.8 %slice-start.1 = ((s8[12582912]{0:T(1024)(128)(4,1)}), s8[4194304]{0:T(1024)(128)(4,1)S(1)}, s32[]{:S(2)}) async-start(s8[12582912]{0:T(1024)(128)(4,1)} %bitcast.88), calls=%async_computation.13 | async-start | bytes 8388608
  256.5 12.8 %slice-start.2 = ((s8[12582912]{0:T(1024)(128)(4,1)}), s8[4194304]{0:T(1024)(128)(4,1)S(1)}, s32[]{:S(2)}) async-start(s8[12582912]{0:T(1024)(128)(4,1)} %bitcast.88), calls=%async_computation.14 | async-start | bytes 8388608
  287.7 315.6 %reduce-scatter.8.cloned.1.call-start = ((), (), s32[]{:S(2)}) async-start(), calls=%async_computation.9 | async-start | bytes 9732096 | tf_op jit(solution)/shard_map/reduce_scatter | solution.py:210
  311.1 292.2 %copy-start.22 = (s32[512,512]{0,1:T(8,128)S(1)}, s32[512,512]{0,1:T(8,128)}, u32[]{:S(2)}) copy-start(s32[512,512]{0,1:T(8,128)} %copy-done.21) | copy-start | bytes 3145732
  311.2 359.6 %all-gather.16.cloned.1.call-start = ((), (), s32[]{:S(2)}) async-start(), calls=%async_computation.8 | async-start | bytes 1327104 | tf_op jit(solution)/shard_map/all_gather | solution.py:213
  350.0 338.0 %all-gather.14.cloned.1.call-start = ((), (), s32[]{:S(2)}) async-start(), calls=%async_computation.7 | async-start | bytes 1327104 | tf_op jit(solution)/shard_map/all_gather | solution.py:213
  461.9 278.8 %all-gather.18.cloned.1.call-start = ((), (), s32[]{:S(2)}) async-start(), calls=%async_computation.10 | async-start | bytes 2654208 | tf_op jit(solution)/shard_map/all_gather | solution.py:213
  611.9 48.7 %copy-start.49 = (f32[512]{0:T(512)S(1)}, f32[512]{0:T(512)}, u32[]{:S(2)}) copy-start(f32[512]{0:T(512)} %copy-done.48) | copy-start | bytes 6148
  611.9 48.7 %copy-start.32 = (bf16[512,768]{1,0:T(8,128)(2,1)S(1)}, bf16[512,768]{1,0:T(8,128)(2,1)}, u32[]{:S(2)}) copy-start(bf16[512,768]{1,0:T(8,128)(2,1)} %param.19) | copy-start | bytes 2359300
  (55 other events, 228.6 us)
Sparse Core Ops, SparseCore 0:
  10.2 33.7 all-gather.7
  46.1 44.1 all-gather.9
  91.8 64.2 all-gather.11
  241.9 108.0 reduce-scatter.9
  355.3 106.5 reduce-scatter.5
  467.7 135.6 reduce-scatter.7
  605.5 40.3 all-gather.15
  648.0 39.9 all-gather.13
  690.2 50.4 all-gather.17

commit v2 on v1

--- a/solution.py
+++ b/solution.py
@@ -53,10 +53,12 @@
     bucket = 16 * (relative > 0).astype(jnp.int32)
     for edge_len in EDGES:
         bucket = bucket + (distance >= edge_len).astype(jnp.int32)
-    onehot = (bucket[:, :, None] == jnp.arange(BUCKETS, dtype=jnp.int32)[None, None, :]).astype(
-        jnp.bfloat16
-    )
-    bias_block = jnp.einsum("qkb,bh->hqk", onehot, rel_table, preferred_element_type=jnp.float32)
+    onehot = (
+        bucket.reshape(1, -1) == jnp.arange(BUCKETS, dtype=jnp.int32)[:, None]
+    ).astype(jnp.bfloat16)
+    bias_block = lax.dot_general(
+        rel_table, onehot, (((0,), (0,)), ((), ())), preferred_element_type=jnp.float32
+    ).reshape(HEADS, block_rows, key_count)
     allowed = (key_pos[None, :] <= query_pos[:, None]) | (piece_ids[None, :] == piece_ids[:, None])
     return (onehot, bias_block, allowed)
 
@@ -113,8 +115,11 @@
         "hqk,qhd->khd", prob_low, grad_block, preferred_element_type=jnp.float32
     )
     if onehot is not None:
-        table_grad = jnp.einsum(
-            "hqk,qkb->bh", grad_scores, onehot, preferred_element_type=jnp.float32
+        table_grad = lax.dot_general(
+            onehot,
+            grad_scores.reshape(HEADS, -1),
+            (((1,), (1,)), ((), ())),
+            preferred_element_type=jnp.float32,
         )
     key_low = key_grad.reshape(key_count, HEADS * HEAD_DIM).astype(jnp.bfloat16)
     value_low = value_grad.reshape(key_count, HEADS * HEAD_DIM).astype(jnp.bfloat16)
@@ -207,10 +212,9 @@
         layer_out = (after_cross + product(inner, down_full)).astype(jnp.bfloat16)
 
         def reduce_rows(packed):
-            owned = lax.psum_scatter(
+            return lax.psum_scatter(
                 packed.astype(jnp.bfloat16), ("fsdp", "replica"), scatter_dimension=0, tiled=True
             )
-            return lax.all_gather(owned, "replica", axis=0, tiled=True)
 
         downproj_grad = left_product(inner, output_grad)
         inner_grad = right_product(output_grad, down_full)
@@ -220,7 +224,7 @@
             [gate_grad.astype(jnp.bfloat16), upper_grad.astype(jnp.bfloat16)], axis=1
         )
         gate_up_grad = left_product(normed_three, gate_upper_low)
-        ffn_owned = reduce_rows(
+        ffn_part = reduce_rows(
             jnp.concatenate([gate_up_grad, downproj_grad.reshape(width, ff_width)], axis=1)
         )
         normed_grad = right_product(gate_upper_low, gate_up)
@@ -236,9 +240,6 @@
         crossquery_grad = left_product(normed_two, query_back)
         kv_back = jnp.concatenate([key_back, value_back], axis=1)
         crosskv_grad = left_product(encoder_states, kv_back)
-        cross_owned = reduce_rows(
-            jnp.concatenate([crossproj_grad, crossquery_grad, crosskv_grad], axis=1)
-        )
         encoder_grad = right_product(kv_back, cross_kv)
         normed_grad = right_product(query_back, cross_query)
         norm_value, pull_norm = jax.vjp(rms_scale, after_self, gain_two.astype(jnp.float32))
@@ -252,25 +253,46 @@
         )
         qkv_back = jnp.concatenate([query_back, key_back, value_back], axis=1)
         selfqkv_grad = left_product(normed_one, qkv_back)
-        self_owned = reduce_rows(jnp.concatenate([selfproj_grad, selfqkv_grad], axis=1))
         normed_grad = right_product(qkv_back, self_full)
         norm_value, pull_norm = jax.vjp(rms_scale, resid_in, gain_one.astype(jnp.float32))
         back_resid, gainself_grad = pull_norm(normed_grad)
         hidden_grad = resid_grad + back_resid
 
-        small_sum = lax.psum(
+        table_block_rows = table_rows
+        table_cols = jnp.pad(
+            reltable_grad.reshape(fsdp_size, table_block_rows, HEADS),
+            ((0, 0), (0, shard_rows - table_block_rows), (0, 0)),
+        ).reshape(width, HEADS)
+        extra = jnp.concatenate(
+            [
+                gainffn_grad[:, None],
+                gaincross_grad[:, None],
+                gainself_grad[:, None],
+                table_cols,
+                jnp.zeros((width, 128 - 3 - HEADS), jnp.float32),
+            ],
+            axis=1,
+        )
+        attn_part = reduce_rows(
             jnp.concatenate(
-                [gainself_grad, gaincross_grad, gainffn_grad, reltable_grad.reshape(-1)]
-            ),
-            ("fsdp", "replica"),
-        )
-        me = lax.axis_index("fsdp")
-        gain_block = lambda i: lax.dynamic_slice_in_dim(
-            small_sum, i * width + me * shard_rows, shard_rows
-        )
-        table_block = lax.dynamic_slice_in_dim(
-            small_sum[3 * width :].reshape(-1, HEADS), me * table_rows, table_rows
-        )
+                [
+                    crossproj_grad,
+                    crossquery_grad,
+                    crosskv_grad,
+                    selfproj_grad,
+                    selfqkv_grad,
+                    extra,
+                ],
+                axis=1,
+            )
+        )
+        owned = lax.all_gather(
+            jnp.concatenate([ffn_part, attn_part], axis=1), "replica", axis=0, tiled=True
+        )
+        ffn_owned = owned[:, : 3 * ff_width]
+        cross_owned = owned[:, 3 * ff_width : 3 * ff_width + 4 * width]
+        self_owned = owned[:, 3 * ff_width + 4 * width : 3 * ff_width + 8 * width]
+        extra_owned = owned[:, 3 * ff_width + 8 * width :].astype(jnp.float32)
 
         as_f32 = lambda v: v.astype(jnp.float32)
         return (
@@ -288,10 +310,10 @@
             as_f32(ffn_owned[:, 0:ff_width]),
             as_f32(ffn_owned[:, ff_width : 2 * ff_width]),
             as_f32(ffn_owned[:, 2 * ff_width :].reshape(-1, width)),
-            gain_block(0),
-            gain_block(1),
-            gain_block(2),
-            table_block,
+            extra_owned[:, 2],
+            extra_owned[:, 1],
+            extra_owned[:, 0],
+            extra_owned[:table_block_rows, 3 : 3 + HEADS],
         )
 
     return on_device

time: 761 us -> 609 us (0.80)
  waiting for transfers between devices: 357 us -> 233 us
  blocking collectives: 50.2 us -> 9.29 us
  matrix products: 149 us -> 159 us
    reduce_scatter x3 -> x1, waiting for transfers between devices: 292 us -> 0.02 us  [reduce_rows(): lax.psum_scatter(packed.astype(jnp.bfloat16), ('fsdp', 'replica'), scatte...]
    unnamed x9 -> x7, waiting for transfers between devices: 0.15 us -> 132 us
    eq x1 -> x0, local copies, waits for them, and re-layouts: 45.9 us -> none  [block_terms(): bucket[:, :, None] == jnp.arange(BUCKETS, dtype=jnp.int32)[None, None, :]]
    psum x1 -> x0, blocking collectives: 40.9 us -> none  [on_device(): lax.psum(jnp.concatenate([gainself_grad, gaincross_grad, gainffn_grad, re...]
    all_gather x1, waiting for transfers between devices: 0.02 us -> 31.7 us  [on_device(): ffn_full = lax.all_gather(ffn_packed, 'fsdp', axis=0, tiled=True)]
    concatenate x0 -> x1, local copies, waits for them, and re-layouts: none -> 14.7 us  [on_device(): jnp.concatenate([crossproj_grad, crossquery_grad, crosskv_grad, selfproj_...]
    convert_element_type x0 -> x1, local copies, waits for them, and re-layouts: none -> 8.91 us  [attend_backward(): grad_scores = (probs * (grad_probs - inner_sum)).astype(jnp.bfloat16)]
    eq x1, other arithmetic: 8.69 us -> 0.58 us  [block_terms(): bucket.reshape(1, -1) == jnp.arange(BUCKETS, dtype=jnp.int32)[:, None]]
  transfers between devices with their start and end apart: 9 -> 6, of which waited for: 5 -> 3; matrix products, arithmetic and copies ran while one was open for 31% -> 43% of each run, Pallas kernels for 0% -> 0%
where the time goes in v2:
time: 609 us; the launch traced here: 603 us
  waiting for transfers between devices  233 us (38%)
  matrix products  159 us (26%)
  local copies, waits for them, and re-layouts  122 us (20%)
  other arithmetic  62.4 us (10%)
  between operations  16.3 us (3%)
  blocking collectives  9.29 us (2%)
    unnamed x7, waiting for transfers between devices  132 us
    all_gather x1, waiting for transfers between devices, on_device(): lax.all_gather(jnp.concatenate([ffn_part, attn_part], axis=1), 'replica',...  69.1 us
    all_gather x1, waiting for transfers between devices, on_device(): ffn_full = lax.all_gather(ffn_packed, 'fsdp', axis=0, tiled=True)  31.7 us
    dot_general x7, matrix products, right_product(): lax.dot_general(left, right, (((1,), (1,)), ((), ())), preferred_element_...  28.9 us
    dot_general x7, matrix products, product(): return jnp.dot(left, right, preferred_element_type=jnp.float32)  28.2 us
    unnamed x166, local copies, waits for them, and re-layouts  26.5 us
    dot_general x2, matrix products, attend_backward(): jnp.einsum('qhd,khd->hqk', grad_block, value_heads, preferred_element_typ...  24.4 us
    dot_general x7, matrix products, left_product(): lax.dot_general(left, right, (((0,), (0,)), ((), ())), preferred_element_...  19.8 us
  transfers between devices with their start and end apart: 6, of which 3 were waited for; matrix products, arithmetic and copies ran while one was open for 43% of the time, Pallas kernels for 0%

profile of v2, /device:TPU:0, one launch (start us, length us, event | category | flops | bytes accessed | tf_op | source)
XLA Modules:
  0.0 602.6 jit_solution(11048088767285036127)
XLA Ops:
  22.0 9.3 %all-reduce.1 = bf16[2688]{0:T(1024)(128)(2,1)S(1)} all-reduce(bf16[2688]{0:T(1024)(128)(2,1)S(1)} %dynamic-update-slice), channel_id=2, replica_groups=mesh['fsdp'=4,'replica'=8] {'fsdp'}, use_global_device_ids=true, to_apply=%add.1 | all-reduce | flops 2688 | bytes 10752
  47.3 9.6 %fusion.1 = f32[12,512,512]{2,0,1:T(8,128)} fusion(s32[512,512]{1,0:T(8,128)S(1)} %convert_add_fusion.1, bf16[32,12]{1,0:T(8,128)(2,1)S(1)} %reshape.429), kind=kOutput, calls=%fused_computation.2 | convolution fusion | flops 209715200 | bytes 13632256 | tf_op jit(solution)/shard_map/dot_general | solution.py:59
  56.8 17.9 %copy.117 = f32[12,512,512]{1,2,0:T(8,128)} copy(f32[12,512,512]{2,0,1:T(8,128)} %fusion.1) | data formatting | bytes 25165824 | tf_op jit(solution)/shard_map/dot_general | solution.py:59
  85.5 6.4 %fusion.102 = (f32[12,512]{1,0:T(8,128)S(1)}, f32[12,512,512]{1,2,0:T(8,128)S(1)}) fusion(f32[12,512,512]{1,2,0:T(8,128)} %copy.117, bf16[512,12,64]{0,2,1:T(8,128)(2,1)S(1)} %bitcast.116, bf16[512,12,64]{0,2,1:T(8,128)(2,1)S(1)} %bitcast.108, pred[512,512]{0,1:T(8,128)(4,1)S(1)} %fusion.74), kind=kOutput, calls=%fused_computation.198 | convolution fusion | flops 412084224 | bytes 27025408 | tf_op jit(solution)/shard_map/qhd,khd->hqk/dot_general | solution.py:67
  123.8 31.7 %all-gather.10.cloned.1.call-done = bf16[768,6144]{1,0:T(8,128)(2,1)} async-done(((bf16[192,6144]{1,0:T(8,128)(2,1)}), bf16[768,6144]{1,0:T(8,128)(2,1)}) %all-gather.10.cloned.1.call-update) | async-done | bytes 9437200 | tf_op jit(solution)/shard_map/all_gather | solution.py:167
  159.5 6.7 %reshape_reshape.3 = bf16[2048,768]{1,0:T(8,128)(2,1)} reshape(bf16[768,2048]{1,0:T(8,128)(2,1)} %slice.162) | data formatting | bytes 6291456 | tf_op jit(solution)/shard_map/reshape;reshape | solution.py:183
  166.2 8.7 %fusion.22 = f32[512,4096]{1,0:T(8,128)} fusion(bf16[768,6144]{1,0:T(8,128)(2,1)} %all-gather.10.cloned.1.call-done, f32[512,768]{1,0:T(8,128)S(1)} %copy-done.10, f32[768]{0:T(1024)S(1)} %reshape.441, f32[512]{0:T(512)S(1)} %fusion.93), kind=kOutput, calls=%fused_computation.35 | convolution fusion | flops 3222405120 | bytes 16258048 | tf_op jit(solution)/shard_map/dot_general | solution.py:26
  175.0 7.6 %fusion.30 = (bf16[512,2048]{1,0:T(8,128)(2,1)S(1)}, bf16[512,2048]{1,0:T(8,128)(2,1)S(1)}, bf16[512,2048]{1,0:T(8,128)(2,1)S(1)}) fusion(f32[512,4096]{1,0:T(8,128)} %fusion.22, bf16[2048,768]{1,0:T(8,128)(2,1)S(1)} %copy-done.27, bf16[512,768]{1,0:T(8,128)(2,1)S(1)} %copy-done.43), kind=kOutput, calls=%fused_computation.45 | convolution fusion | flops 1637875712 | bytes 18612224 | tf_op jit(solution)/shard_map/dot_general | solution.py:36
  182.7 5.8 convolution_convert_fusion
  196.7 6.6 %reshape.436 = bf16[768,2048]{1,0:T(8,128)(2,1)} reshape(bf16[2048,768]{1,0:T(8,128)(2,1)} %convolution_convert_fusion.3) | data formatting | bytes 6291456 | tf_op jit(solution)/shard_map/reshape | solution.py:228
  203.3 9.1 %pad_maximum_fusion = bf16[768,6144]{1,0:T(8,128)(2,1)} fusion(bf16[768,2048]{1,0:T(8,128)(2,1)} %reshape.436, bf16[768,4096]{1,0:T(8,128)(2,1)} %convolution_convert_fusion), kind=kLoop, calls=%fused_computation.23 | loop fusion | flops 18874368 | bytes 18874368 | tf_op jit(solution)/shard_map/concatenate | solution.py:228
  225.9 13.6 %multiply_reduce_fusion.1 = (f32[12,512]{1,0:T(8,128)S(1)}, f32[12,512,512]{1,2,0:T(8,128)}) fusion(f32[12,512,512]{1,2,0:T(8,128)} %copy-done.2, f32[12,512]{1,0:T(8,128)S(1)} %log_add_fusion.1, bf16[512,12,64]{0,2,1:T(8,128)(2,1)} %bitcast.112, bf16[512,12,64]{0,2,1:T(8,128)(2,1)} %bitcast.130), kind=kOutput, calls=%fused_computation.12 | convolution fusion | flops 412084224 | bytes 26787840 | tf_op jit(solution)/shard_map/qhd,khd->hqk/dot_general | solution.py:102
  239.6 7.3 %multiply_convert_fusion.1 = bf16[12,512,512]{1,2,0:T(8,128)(2,1)S(1)} fusion(f32[12,512,512]{1,2,0:T(8,128)} %get-tuple-element.59, f32[12,512,512]{1,2,0:T(8,128)S(1)} %bitcast.107, f32[12,512]{1,0:T(8,128)S(1)} %get-tuple-element.58, f32[12,512]{1,0:T(8,128)S(1)} %log_add_fusion.1), kind=kLoop, calls=%fused_computation.11 | loop fusion | flops 12582912 | bytes 31506432 | tf_op jit(solution)/shard_map/convert_element_type | solution.py:106
  269.9 7.0 %fusion.46 = bf16[12,64,512]{2,1,0:T(8,128)(2,1)S(1)} fusion(bf16[512,12,64]{0,2,1:T(8,128)(2,1)S(1)} %bitcast.113, f32[12,512,512]{1,2,0:T(8,128)} %copy-done.2, f32[12,512]{1,0:T(8,128)S(1)} %copy-done.50), kind=kOutput, calls=%fused_computation.104 | convolution fusion | flops 409337856 | bytes 14180352 | tf_op jit(solution)/shard_map/hqk,qhd->khd/dot_general | solution.py:114
  284.9 10.8 %multiply_reduce_fusion = (f32[12,512]{1,0:T(8,128)S(1)}, f32[12,512,512]{1,2,0:T(8,128)}) fusion(f32[12,512,512]{1,2,0:T(8,128)} %copy-done.1, f32[12,512]{1,0:T(8,128)S(1)} %copy-done.48, bf16[512,12,64]{0,2,1:T(8,128)(2,1)S(1)} %bitcast.114, bf16[512,12,64]{0,2,1:T(8,128)(2,1)} %bitcast.128), kind=kOutput, calls=%fused_computation.9 | convolution fusion | flops 412084224 | bytes 26787840 | tf_op jit(solution)/shard_map/qhd,khd->hqk/dot_general | solution.py:102
  298.1 9.7 %multiply_convert_fusion = bf16[12,512,512]{1,2,0:T(8,128)(2,1)} fusion(f32[12,512,512]{1,2,0:T(8,128)} %get-tuple-element.62, f32[12,512,512]{1,2,0:T(8,128)S(1)} %bitcast.105, f32[12,512]{1,0:T(8,128)S(1)} %get-tuple-element.61, f32[12,512]{1,0:T(8,128)S(1)} %copy-done.48), kind=kLoop, calls=%fused_computation.8 | loop fusion | flops 12582912 | bytes 31506432 | tf_op jit(solution)/shard_map/convert_element_type | solution.py:106
  307.8 8.9 %copy.130 = bf16[12,512,512]{2,1,0:T(8,128)(2,1)} copy(bf16[12,512,512]{1,2,0:T(8,128)(2,1)} %multiply_convert_fusion) | data formatting | bytes 12582912 | tf_op jit(solution)/shard_map/convert_element_type | solution.py:106
  316.8 5.2 convolution_convert_fusion.13
  323.2 7.0 %fusion.49 = bf16[12,64,512]{2,1,0:T(8,128)(2,1)S(1)} fusion(bf16[512,12,64]{0,2,1:T(8,128)(2,1)S(1)} %bitcast.115, f32[12,512,512]{1,2,0:T(8,128)} %copy-done.1, f32[12,512]{1,0:T(8,128)S(1)} %copy-done.48), kind=kOutput, calls=%fused_computation.105 | convolution fusion | flops 409337856 | bytes 14180352 | tf_op jit(solution)/shard_map/hqk,qhd->khd/dot_general | solution.py:114
  334.5 8.1 %reshape.476 = bf16[12,262144,1]{1,0,2:T(8,128)(2,1)} reshape(bf16[12,512,512]{2,1,0:T(8,128)(2,1)} %copy.130) | data formatting | bytes 12582912 | tf_op jit(solution)/shard_map/reshape | solution.py:120
  342.7 7.5 %fusion.54 = bf16[4,8,12]{2,1,0:T(8,128)(2,1)S(1)} fusion(bf16[12,262144,1]{1,0,2:T(8,128)(2,1)} %reshape.476, s32[4,8]{1,0:T(4,128)S(1)} %copy-done.59, s32[262144]{0:T(1024)S(1)} %copy-done.36), kind=kOutput, calls=%fused_computation.112 | convolution fusion | flops 209715584 | bytes 7340928 | tf_op jit(solution)/shard_map/dot_general | solution.py:118
  355.7 14.7 %concatenate.40 = bf16[768,6272]{1,0:T(8,128)(2,1)} concatenate(bf16[768,768]{1,0:T(8,128)(2,1)S(1)} %copy-done.18, bf16[768,768]{1,0:T(8,128)(2,1)} %copy.132, bf16[768,1536]{1,0:T(8,128)(2,1)} %copy.133, bf16[768,768]{1,0:T(8,128)(2,1)} %copy.134, bf16[768,2304]{1,0:T(8,128)(2,1)} %convolution_convert_fusion.1, bf16[768,1]{1,0:T(8,128)(2,1)} %broadcast_in_dim.42, ...), dimensions={1} | concatenate | bytes 19267584 | tf_op jit(solution)/shard_map/concatenate | solution.py:277
  370.5 131.9 %reduce-scatter.7.cloned.1.call-done = bf16[24,6272]{1,0:T(8,128)(2,1)} async-done(((bf16[768,6272]{1,0:T(8,128)(2,1)}), bf16[24,6272]{1,0:T(8,128)(2,1)}) %reduce-scatter.7.cloned.1.call-update) | async-done | bytes 301072
  514.6 69.1 %all-gather.12.cloned.1.call-done = bf16[192,12416]{1,0:T(8,128)(2,1)} async-done(((bf16[24,12416]{1,0:T(8,128)(2,1)}), bf16[192,12416]{1,0:T(8,128)(2,1)}) %all-gather.12.cloned.1.call-update) | async-done | bytes 4767760 | tf_op jit(solution)/shard_map/all_gather | solution.py:289
  (271 shorter events, 166.1 us)
Async XLA Ops:
  7.2 99.7 %copy-start = (bf16[512,768]{1,0:T(8,128)(2,1)S(1)}, bf16[512,768]{1,0:T(8,128)(2,1)}, u32[]{:S(2)}) copy-start(bf16[512,768]{1,0:T(8,128)(2,1)} %param.20) | copy-start | bytes 2359300
  7.2 70.6 %all-gather.6.cloned.1.call-start = ((), (), s32[]{:S(2)}) async-start(), calls=%async_computation.2 | async-start | bytes 4423680 | tf_op jit(solution)/shard_map/all_gather | solution.py:164
  9.6 90.3 %all-gather.8.cloned.1.call-start = ((), (), s32[]{:S(2)}) async-start(), calls=%async_computation.3 | async-start | bytes 7372800 | tf_op jit(solution)/shard_map/all_gather | solution.py:166
  14.8 140.7 %all-gather.10.cloned.1.call-start = ((), (), s32[]{:S(2)}) async-start(), calls=%async_computation.4 | async-start | bytes 11796480 | tf_op jit(solution)/shard_map/all_gather | solution.py:167
  19.7 350.8 %reduce-scatter.5.cloned.1.call-start = ((), (), s32[]{:S(2)}) async-start(), calls=%async_computation.5 | async-start | bytes 9732096 | tf_op jit(solution)/shard_map/reduce_scatter | solution.py:215
  37.3 40.5 %copy-start.56 = (f32[512]{0:T(512)}, f32[512]{0:T(512)S(1)}, u32[]{:S(2)}) copy-start(f32[512]{0:T(512)S(1)} %fusion.91) | copy-start | bytes 6148
  38.1 39.7 %copy-start.54 = (f32[768]{0:T(1024)}, f32[768]{0:T(1024)S(1)}, u32[]{:S(2)}) copy-start(f32[768]{0:T(1024)S(1)} %reshape.439) | copy-start | bytes 9220
  56.8 17.9 %copy-start.21 = (s32[64,4,8,128]{3,1,2,0:T(4,128)S(1)}, s32[64,4,8,128]{3,1,2,0:T(4,128)}, u32[]{:S(2)}) copy-start(s32[64,4,8,128]{3,1,2,0:T(4,128)} %copy.149) | copy-start | bytes 3145732
  56.8 17.9 %copy-start.22 = (s32[64,4,8,128]{3,1,2,0:T(4,128)S(1)}, s32[64,4,8,128]{3,1,2,0:T(4,128)}, u32[]{:S(2)}) copy-start(s32[64,4,8,128]{3,1,2,0:T(4,128)} %copy.150) | copy-start | bytes 3145732
  103.0 17.3 %copy-start.7 = (f32[512,768]{1,0:T(8,128)}, f32[512,768]{1,0:T(8,128)S(1)}, u32[]{:S(2)}) copy-start(f32[512,768]{1,0:T(8,128)S(1)} %get-tuple-element.52) | copy-start | bytes 4718596
  123.8 115.7 %copy-start.49 = (f32[12,512]{1,0:T(8,128)}, f32[12,512]{1,0:T(8,128)S(1)}, u32[]{:S(2)}) copy-start(f32[12,512]{1,0:T(8,128)S(1)} %log_add_fusion.1) | copy-start | bytes 73732
  166.2 22.2 %slice-start.6 = ((s8[9437184]{0:T(1024)(128)(4,1)}), s8[4194304]{0:T(1024)(128)(4,1)S(1)}, s32[]{:S(2)}) async-start(s8[9437184]{0:T(1024)(128)(4,1)} %bitcast.135), calls=%async_computation.14 | async-start | bytes 8388608
  175.0 13.5 %slice-start.7 = ((s8[9437184]{0:T(1024)(128)(4,1)}), s8[4194304]{0:T(1024)(128)(4,1)S(1)}, s32[]{:S(2)}) async-start(s8[9437184]{0:T(1024)(128)(4,1)} %bitcast.135), calls=%async_computation.15 | async-start | bytes 8388608
  175.0 13.5 %slice-start.8 = ((s8[9437184]{0:T(1024)(128)(4,1)}), s8[1048576]{0:T(1024)(128)(4,1)S(1)}, s32[]{:S(2)}) async-start(s8[9437184]{0:T(1024)(128)(4,1)} %bitcast.135), calls=%async_computation.16 | async-start | bytes 2097152
  212.4 290.0 %reduce-scatter.7.cloned.1.call-start = ((), (), s32[]{:S(2)}) async-start(), calls=%async_computation.7 | async-start | bytes 9934848
  225.9 13.6 %slice-start.3 = ((s8[12582912]{0:T(1024)(128)(4,1)}), s8[4194304]{0:T(1024)(128)(4,1)S(1)}, s32[]{:S(2)}) async-start(s8[12582912]{0:T(1024)(128)(4,1)} %bitcast.106), calls=%async_computation.11 | async-start | bytes 8388608
  225.9 13.6 %slice-start.4 = ((s8[12582912]{0:T(1024)(128)(4,1)}), s8[4194304]{0:T(1024)(128)(4,1)S(1)}, s32[]{:S(2)}) async-start(s8[12582912]{0:T(1024)(128)(4,1)} %bitcast.106), calls=%async_computation.12 | async-start | bytes 8388608
  225.9 13.6 %slice-start.5 = ((s8[12582912]{0:T(1024)(128)(4,1)}), s8[4194304]{0:T(1024)(128)(4,1)S(1)}, s32[]{:S(2)}) async-start(s8[12582912]{0:T(1024)(128)(4,1)} %bitcast.106), calls=%async_computation.13 | async-start | bytes 8388608
  284.9 10.8 %slice-start = ((s8[12582912]{0:T(1024)(128)(4,1)}), s8[4194304]{0:T(1024)(128)(4,1)S(1)}, s32[]{:S(2)}) async-start(s8[12582912]{0:T(1024)(128)(4,1)} %bitcast.104), calls=%async_computation.8 | async-start | bytes 8388608
  284.9 12.0 %slice-start.1 = ((s8[12582912]{0:T(1024)(128)(4,1)}), s8[4194304]{0:T(1024)(128)(4,1)S(1)}, s32[]{:S(2)}) async-start(s8[12582912]{0:T(1024)(128)(4,1)} %bitcast.104), calls=%async_computation.9 | async-start | bytes 8388608
  284.9 13.2 %slice-start.2 = ((s8[12582912]{0:T(1024)(128)(4,1)}), s8[4194304]{0:T(1024)(128)(4,1)S(1)}, s32[]{:S(2)}) async-start(s8[12582912]{0:T(1024)(128)(4,1)} %bitcast.104), calls=%async_computation.10 | async-start | bytes 8388608
  370.4 134.0 %copy-start.53 = (f32[512]{0:T(512)S(1)}, f32[512]{0:T(512)}, u32[]{:S(2)}) copy-start(f32[512]{0:T(512)} %copy-done.52) | copy-start | bytes 6148
  370.4 134.0 %copy-start.32 = (bf16[512,768]{1,0:T(8,128)(2,1)S(1)}, bf16[512,768]{1,0:T(8,128)(2,1)}, u32[]{:S(2)}) copy-start(bf16[512,768]{1,0:T(8,128)(2,1)} %param.19) | copy-start | bytes 2359300
  370.4 213.3 %all-gather.12.cloned.1.call-start = ((), (), s32[]{:S(2)}) async-start(), calls=%async_computation.6 | async-start | bytes 5363712 | tf_op jit(solution)/shard_map/all_gather | solution.py:289
  (59 other events, 316.0 us)
Sparse Core Ops, SparseCore 0:
  9.7 33.7 all-gather.5
  45.6 44.1 all-gather.7
  91.3 64.2 all-gather.9
  212.5 136.2 reduce-scatter.4
  370.6 131.8 reduce-scatter.6
  505.0 78.6 all-gather.11
